TPU v7x, 32 devices: a whole 2x2x4 slice. The times are simulated.
32 devices in a mesh: dp: 8 (over z, x), mp: 4 (over y, core).
Axes of the slice: x: 2, y: 2, z: 4, core: 2. Of those that a mesh axis runs over, the one named last changes fastest.
Arguments:
- tokens: bfloat16 [64, 256, 768], P(('dp', 'mp')), may hold values from -6 to 6
- cotangent: bfloat16 [64, 256, 768], P(('dp', 'mp')), may hold values from -6 to 6
- segment_ids: int32 [64, 256], P('dp'), may hold values from 0 to 32, as said below
- live_mask: int32 [64, 256], P('dp'), may hold values from 0 to 1, as said below
- expert_ids: int32 [64], P('dp'), may hold values from 0 to 1, as said below
- qkv_weight: bfloat16 [768, 3, 768], P(None, None, 'mp'), may hold values from -0.21875 to 0.21875
- out_weight: bfloat16 [768, 768], P('mp'), may hold values from -0.875 to 0.875
- in_weight: bfloat16 [2, 768, 3072], P(None, None, 'mp'), may hold values from -0.21875 to 0.21875
- down_weight: bfloat16 [2, 3072, 768], P(None, 'mp'), may hold values from -0.15625 to 0.15625
- gain_attn: float32 [768], replicated, may hold values from 0.5 to 1.5
- shift_attn: float32 [768], replicated, may hold values from -3 to 3
- gain_ffn: float32 [768], replicated, may hold values from 0.5 to 1.5
- shift_ffn: float32 [768], replicated, may hold values from -3 to 3
Outputs:
- output: bfloat16 [64, 256, 768], P(('dp', 'mp'))
- grad_tokens: float32 [64, 256, 768], P(('dp', 'mp'))
- counts: int32 [2], replicated
- grad_qkv_weight: float32 [768, 3, 768], P(None, None, 'mp')
- grad_out_weight: float32 [768, 768], P('mp')
- grad_in_weight: float32 [2, 768, 3072], P(None, None, 'mp')
- grad_down_weight: float32 [2, 3072, 768], P(None, 'mp')
- grad_gain_attn: float32 [768], replicated
- grad_shift_attn: float32 [768], replicated
- grad_gain_ffn: float32 [768], replicated
- grad_shift_ffn: float32 [768], replicated
Inputs may be any that keep to these rules, and one draw needn't show every extreme that they name: `segment_ids`: ids never fall along a row; the live slots with one id form one caption of 8 to 40 tokens, and captions of both lengths occur; padding slots carry the id 32. `live_mask`: each row is 1 on its first live slots and 0 on the padding after them; every row has live slots. `expert_ids`: every expert is named by some row.
All inputs are finite; a program needn't handle non-finite values.
Results may differ from a plain program's by a relative error of at most 0.018.
Values may be sent and summed in bfloat16 or wider, within the bound.
No kernel may reach another device: no remote copies, remote signals or barrier semaphores. Data moves between devices by JAX's collectives and lax.ppermute only.
A program may use at most 128 MiB of HBM per device.

v0:
```python
import jax
import jax.numpy as jnp
from jax import lax
from jax.sharding import PartitionSpec as P

HD = 64


norm_epsilon = 1e-05
masked_fill = -1e30


def layer_norm(values, norm_gain, norm_shift):
    average = jnp.mean(values, axis=-1, keepdims=True)
    centred = values - average
    variance = jnp.mean(centred * centred, axis=-1, keepdims=True)
    return centred * lax.rsqrt(variance + norm_epsilon) * norm_gain + norm_shift


def gelu_exact(values):
    return jax.nn.gelu(values, approximate=False)


def select_rows(values, hot_column):
    return values * hot_column[:, None, None]


def per_device(
    tokens,
    cotangent,
    segment_ids,
    live_mask,
    expert_ids,
    qkv_weight,
    out_weight,
    in_weight,
    down_weight,
    gain_attn,
    shift_attn,
    gain_ffn,
    shift_ffn,
):
    local_rows, slots, model_width = tokens.shape
    experts = in_weight.shape[0]
    heads_local = qkv_weight.shape[2] // HD
    score_scale = HD ** (-0.5)
    first_row = lax.axis_index("mp") * local_rows
    expert_hot = expert_ids[:, None] == jnp.arange(experts)[None, :]
    row_live = jnp.sum(live_mask, axis=1)
    local_counts = jnp.sum(jnp.where(expert_hot, row_live[:, None], 0), axis=0)
    counts = lax.psum(local_counts, "dp")
    hot_matrix = expert_hot.astype(jnp.bfloat16)
    token_float = tokens.astype(jnp.float32)
    norm_one = layer_norm(token_float, gain_attn, shift_attn).astype(jnp.bfloat16)
    norm_one_full = lax.all_gather(norm_one, "mp", axis=0, tiled=True)
    qkv_flat = qkv_weight.reshape(model_width, -1)
    qkv_all = jnp.einsum(
        "rsd,dk->rsk", norm_one_full, qkv_flat, preferred_element_type=jnp.float32
    ).astype(jnp.bfloat16)
    group_rows = qkv_all.shape[0]
    qkv_split = qkv_all.reshape(group_rows, slots, 3, heads_local, HD)
    queries = qkv_split[:, :, 0]
    key_part = qkv_split[:, :, 1]
    value_part = qkv_split[:, :, 2]
    same_caption = segment_ids[:, :, None] == segment_ids[:, None, :]
    diagonal = jnp.arange(slots)[:, None] == jnp.arange(slots)[None, :]
    allowed = (same_caption & ((live_mask[:, None, :] == 1) | diagonal[None]))[:, None]

    def masked_scores():
        raw_scores = (
            jnp.einsum("rqhd,rkhd->rhqk", queries, key_part, preferred_element_type=jnp.float32)
            * score_scale
        )
        return jnp.where(allowed, raw_scores, masked_fill)

    scores = masked_scores()
    row_top = jnp.max(scores, axis=-1, keepdims=True)
    exp_scores = jnp.exp(scores - row_top)
    row_total = jnp.sum(exp_scores, axis=-1, keepdims=True)
    attn_probs = exp_scores / row_total
    log_total = row_top + jnp.log(row_total)
    head_mix = jnp.einsum(
        "rhqk,rkhd->rqhd",
        attn_probs.astype(jnp.bfloat16),
        value_part,
        preferred_element_type=jnp.float32,
    )
    head_mix = head_mix.reshape(group_rows, slots, heads_local * HD).astype(jnp.bfloat16)
    picked = head_mix
    attn_local = lax.psum_scatter(
        jnp.einsum("rsk,kd->rsd", picked, out_weight, preferred_element_type=jnp.float32).astype(
            jnp.bfloat16
        ),
        "mp",
        scatter_dimension=0,
        tiled=True,
    ).astype(jnp.float32)
    residual = token_float + attn_local
    norm_two = layer_norm(residual, gain_ffn, shift_ffn).astype(jnp.bfloat16)
    norm_two_full = lax.all_gather(norm_two, "mp", axis=0, tiled=True)
    upward = jnp.zeros((group_rows, slots, in_weight.shape[2]), jnp.float32)
    for expert in range(experts):
        upward = upward + jnp.einsum(
            "rsd,df->rsf",
            select_rows(norm_two_full, hot_matrix[:, expert]),
            in_weight[expert],
            preferred_element_type=jnp.float32,
        )
    activated = gelu_exact(upward).astype(jnp.bfloat16)
    picked = activated
    hot_picked = hot_matrix
    total = jnp.zeros((local_rows * lax.axis_size("mp"), slots, model_width), jnp.float32)
    for ffn_expert in range(experts):
        total = total + jnp.einsum(
            "rsf,fd->rsd",
            select_rows(picked, hot_picked[:, ffn_expert]),
            down_weight[ffn_expert],
            preferred_element_type=jnp.float32,
        )
    ffn_local = lax.psum_scatter(
        total.astype(jnp.bfloat16), "mp", scatter_dimension=0, tiled=True
    ).astype(jnp.float32)
    output = (residual + ffn_local).astype(jnp.bfloat16)
    count_float = counts.astype(jnp.float32)
    loss_weight = jnp.sum(count_float) / (experts * count_float)
    local_hot = lax.dynamic_slice_in_dim(expert_hot, first_row, local_rows, 0)
    row_weight = jnp.sum(jnp.where(local_hot, loss_weight[None, :], 0.0), axis=1)
    live_local = lax.dynamic_slice_in_dim(live_mask, first_row, local_rows, 0)
    grad_output = (
        cotangent.astype(jnp.float32)
        * live_local[:, :, None].astype(jnp.float32)
        * row_weight[:, None, None]
    )
    grad_ffn_full = lax.all_gather(grad_output.astype(jnp.bfloat16), "mp", axis=0, tiled=True)
    grad_act = jnp.zeros(upward.shape, jnp.float32)
    down_list = []
    for expert in range(experts):
        masked_grad = select_rows(grad_ffn_full, hot_matrix[:, expert])
        grad_act = grad_act + jnp.einsum(
            "rsd,fd->rsf", masked_grad, down_weight[expert], preferred_element_type=jnp.float32
        )
        down_list.append(
            jnp.einsum("rsf,rsd->fd", activated, masked_grad, preferred_element_type=jnp.float32)
        )
    grad_down_weight = jnp.stack(down_list, axis=0)
    grad_up = jax.vjp(gelu_exact, upward)[1](grad_act)[0].astype(jnp.bfloat16)
    in_list = []
    for expert in range(experts):
        in_list.append(
            jnp.einsum(
                "rsd,rsf->df",
                select_rows(norm_two_full, hot_matrix[:, expert]),
                grad_up,
                preferred_element_type=jnp.float32,
            )
        )
    grad_in_weight = jnp.stack(in_list, axis=0)
    picked = grad_up
    hot_picked = hot_matrix
    total = jnp.zeros((local_rows * lax.axis_size("mp"), slots, model_width), jnp.float32)
    for expert in range(experts):
        total = total + jnp.einsum(
            "rsf,df->rsd",
            select_rows(picked, hot_picked[:, expert]),
            in_weight[expert],
            preferred_element_type=jnp.float32,
        )
    grad_norm_two = lax.psum_scatter(
        total.astype(jnp.bfloat16), "mp", scatter_dimension=0, tiled=True
    ).astype(jnp.float32)
    second_back = jax.vjp(layer_norm, residual, gain_ffn, shift_ffn)[1]
    grad_from_second, grad_gain_ffn, grad_shift_ffn = second_back(grad_norm_two)
    grad_residual = grad_output + grad_from_second
    grad_attn_full = lax.all_gather(grad_residual.astype(jnp.bfloat16), "mp", axis=0, tiled=True)
    grad_out_weight = jnp.einsum(
        "rsk,rsd->kd", head_mix, grad_attn_full, preferred_element_type=jnp.float32
    )
    grad_mix = jnp.einsum(
        "rsd,kd->rsk", grad_attn_full, out_weight, preferred_element_type=jnp.float32
    )
    grad_mix = grad_mix.astype(jnp.bfloat16).reshape(group_rows, slots, heads_local, HD)
    attn_again = jnp.exp(masked_scores() - log_total)
    grad_probs = jnp.einsum(
        "rqhd,rkhd->rhqk", grad_mix, value_part, preferred_element_type=jnp.float32
    )
    grad_scores = attn_again * (
        grad_probs - jnp.sum(grad_probs * attn_again, axis=-1, keepdims=True)
    )
    grad_scores = grad_scores.astype(jnp.bfloat16)
    grad_value = jnp.einsum(
        "rhqk,rqhd->rkhd",
        attn_again.astype(jnp.bfloat16),
        grad_mix,
        preferred_element_type=jnp.float32,
    )
    grad_query = (
        jnp.einsum("rhqk,rkhd->rqhd", grad_scores, key_part, preferred_element_type=jnp.float32)
        * score_scale
    )
    grad_key = (
        jnp.einsum("rhqk,rqhd->rkhd", grad_scores, queries, preferred_element_type=jnp.float32)
        * score_scale
    )
    grad_qkv = (
        jnp.stack([grad_query, grad_key, grad_value], axis=2)
        .astype(jnp.bfloat16)
        .reshape(group_rows, slots, -1)
    )
    grad_qkv_weight = jnp.einsum(
        "rsd,rsk->dk", norm_one_full, grad_qkv, preferred_element_type=jnp.float32
    )
    grad_qkv_weight = grad_qkv_weight.reshape(qkv_weight.shape)
    picked = grad_qkv
    grad_norm_one = lax.psum_scatter(
        jnp.einsum("rsk,dk->rsd", picked, qkv_flat, preferred_element_type=jnp.float32).astype(
            jnp.bfloat16
        ),
        "mp",
        scatter_dimension=0,
        tiled=True,
    ).astype(jnp.float32)
    first_back = jax.vjp(layer_norm, token_float, gain_attn, shift_attn)[1]
    grad_from_first, grad_gain_attn, grad_shift_attn = first_back(grad_norm_one)
    grad_tokens = grad_residual + grad_from_first
    norm_grads = lax.psum(
        (grad_gain_attn, grad_shift_attn, grad_gain_ffn, grad_shift_ffn), ("dp", "mp")
    )
    summed = lax.psum((grad_qkv_weight, grad_out_weight, grad_in_weight, grad_down_weight), "dp")
    return (
        output,
        grad_tokens,
        counts,
        summed[0],
        summed[1],
        summed[2],
        summed[3],
        norm_grads[0],
        norm_grads[1],
        norm_grads[2],
        norm_grads[3],
    )


def solution(mesh):
    in_specs = (
        P(("dp", "mp"), None, None),
        P(("dp", "mp"), None, None),
        P("dp", None),
        P("dp", None),
        P("dp"),
        P(None, None, "mp"),
        P("mp", None),
        P(None, None, "mp"),
        P(None, "mp", None),
        P(),
        P(),
        P(),
        P(),
    )
    out_specs = (
        P(("dp", "mp"), None, None),
        P(("dp", "mp"), None, None),
        P(),
        P(None, None, "mp"),
        P("mp", None),
        P(None, None, "mp"),
        P(None, "mp", None),
        P(),
        P(),
        P(),
        P(),
    )
    return jax.shard_map(
        per_device, mesh=mesh, in_specs=in_specs, out_specs=out_specs, check_vma=False
    )
```

profile of v0, /device:TPU:0, one launch (start us, length us, event | category | flops | bytes accessed | tf_op | source)
XLA Modules:
  0.0 761.4 jit_solution(12436911673130633448)
XLA Ops:
  7.3 1.4 convert_reduce_fusion.2
  8.6 1.5 fusion.70
  10.2 2.4 fusion.68
  12.7 0.7 or_and_fusion
  13.4 30.5 %all-gather.5.cloned.1.call-done = bf16[8,256,768]{2,1,0:T(8,128)(2,1)} async-done(((bf16[2,256,768]{2,1,0:T(8,128)(2,1)}), bf16[8,256,768]{2,1,0:T(8,128)(2,1)}) %all-gather.5.cloned.1.call-update) | async-done | bytes 3145744 | tf_op jit(solution)/shard_map/all_gather | solution.py:55
  44.0 3.9 convolution_convert_fusion.2
  47.9 1.3 fusion.125
  49.3 1.1 fusion.6
  50.4 1.5 copy-done.2
  51.9 1.2 fusion.95
  53.1 0.9 copy-done.10
  54.0 2.7 convolution_convert_fusion.1
  57.1 11.4 %psum.63 = s32[2]{0:T(128)S(1)} all-reduce(s32[2]{0:T(128)S(1)} %select_reduce_fusion), channel_id=1, replica_groups=mesh['dp'=8,'mp'=4] {'dp'}, use_global_device_ids=true, to_apply=%region_10.11 | all-reduce | flops 2 | bytes 16 | tf_op jit(solution)/shard_map/psum | solution.py:51
  68.4 0.6 convert_reduce_fusion.3
  69.0 0.7 multiply_divide_fusion
  69.8 1.1 fusion.74
  71.0 23.8 %reduce-scatter.5.cloned.1.call-done = bf16[2,256,768]{2,1,0:T(8,128)(2,1)} async-done(((bf16[8,256,768]{2,1,0:T(8,128)(2,1)}), bf16[2,256,768]{2,1,0:T(8,128)(2,1)}) %reduce-scatter.5.cloned.1.call-update) | async-done | bytes 786448 | tf_op jit(solution)/shard_map/reduce_scatter | solution.py:90
  94.8 1.5 fusion.97
  96.3 1.5 multiply_reduce_fusion.1
  97.9 1.3 add_convert_fusion.4
  99.5 26.0 %all-gather.9.cloned.1.call-done = bf16[8,256,768]{2,1,0:T(8,128)(2,1)} async-done(((bf16[2,256,768]{2,1,0:T(8,128)(2,1)}), bf16[8,256,768]{2,1,0:T(8,128)(2,1)}) %all-gather.9.cloned.1.call-update) | async-done | bytes 3145744 | tf_op jit(solution)/shard_map/all_gather | solution.py:134
  125.5 7.5 fusion.24
  133.0 23.0 %all-gather.7.cloned.1.call-done = bf16[8,256,768]{2,1,0:T(8,128)(2,1)} async-done(((bf16[2,256,768]{2,1,0:T(8,128)(2,1)}), bf16[8,256,768]{2,1,0:T(8,128)(2,1)}) %all-gather.7.cloned.1.call-update) | async-done | bytes 3145744 | tf_op jit(solution)/shard_map/all_gather | solution.py:100
  156.0 5.1 fusion.32
  161.1 4.6 fusion.88
  165.7 15.1 %multiply_convert_fusion.1 = (bf16[8,256,768]{2,1,0:T(8,128)(2,1)}, f32[8,256,768]{2,1,0:T(8,128)S(1)}) fusion(f32[8,256,768]{2,1,0:T(8,128)S(1)} %get-tuple-element.39, u8[256,768]{1,0:T(8,128)(4,1)S(1)} %get-tuple-element.12, u8[256,768]{1,0:T(8,128)(4,1)S(1)} %get-tuple-element.11), kind=kLoop, calls=%fused_computation.13 | loop fusion | flops 110100480 | bytes 16121856 | tf_op jit(solution)/shard_map/convert_element_type | solution.py:109
  180.8 10.6 %add_convert_fusion.1 = bf16[8,256,768]{2,1,0:T(8,128)(2,1)} fusion(f32[8,256,768]{2,1,0:T(8,128)S(1)} %get-tuple-element.30, f32[8,256,768]{2,1,0:T(8,128)} %fusion.24, f32[8,256,768]{2,1,0:T(8,128)S(1)} %get-tuple-element.39, bf16[8,256,768]{2,1,0:T(8,128)(2,1)} %all-gather.9.cloned.1.call-done, bf16[8]{0:T(256)(128)(2,1)S(1)} %get-tuple-element.35, ...), kind=kOutput, calls=%fused_computation.11 | convolution fusion | flops 2441084928 | bytes 26345488 | tf_op jit(solution)/shard_map/rsd,fd->rsf/dot_general | solution.py:139
  191.4 4.7 fusion.13
  196.2 4.1 add_convert_fusion
  200.3 38.0 %reduce-scatter.9.cloned.1.call-done = bf16[2,256,768]{2,1,0:T(8,128)(2,1)} async-done(((bf16[8,256,768]{2,1,0:T(8,128)(2,1)}), bf16[2,256,768]{2,1,0:T(8,128)(2,1)}) %reduce-scatter.9.cloned.1.call-update) | async-done | bytes 786448 | tf_op jit(solution)/shard_map/reduce_scatter | solution.py:168
  238.3 1.9 convert_reduce_fusion.1
  240.2 2.2 fusion.72
  242.4 2.8 fusion.115
  245.5 28.4 %all-gather.11.cloned.1.call-done = bf16[8,256,768]{2,1,0:T(8,128)(2,1)} async-done(((bf16[2,256,768]{2,1,0:T(8,128)(2,1)}), bf16[8,256,768]{2,1,0:T(8,128)(2,1)}) %all-gather.11.cloned.1.call-update) | async-done | bytes 3145744 | tf_op jit(solution)/shard_map/all_gather | solution.py:174
  273.9 3.2 convolution_convert_fusion.3
  277.2 4.0 fusion.92
  281.2 5.3 multiply_reduce_fusion
  286.5 4.6 multiply_convert_fusion
  291.1 1.1 multiply_bitcast_fusion
  292.2 0.7 multiply_bitcast_fusion.1
  292.9 0.3 maximum_convert_fusion
  293.1 1.4 copy-done.5
  294.6 0.3 copy.69
  294.9 4.1 convolution_convert_fusion
  299.0 5.1 fusion.17
  304.1 4.1 add_convert_fusion.2
  308.5 5.9 fusion.58
  314.5 2.8 fusion.55
  317.3 0.4 copy-done.22
  317.7 2.8 fusion.64
  320.5 2.8 fusion.61
  323.3 4.4 pad_maximum_fusion
  327.7 1.6 convolution_bitcast_fusion
  329.4 5.4 fusion.89
  334.8 2.2 reduce-scatter.11.cloned.1.call-done
  337.0 1.7 convert_reduce_fusion
  338.7 2.1 fusion.73
  340.8 39.9 %all-reduce = (f32[768]{0:T(1024)}, f32[768]{0:T(1024)}, f32[768]{0:T(1024)}, f32[768]{0:T(1024)}) all-reduce(f32[768]{0:T(1024)S(1)} %get-tuple-element.15, f32[768]{0:T(1024)S(1)} %get-tuple-element.19, f32[768]{0:T(1024)S(1)} %get-tuple-element.13, f32[768]{0:T(1024)S(1)} %get-tuple-element.17), channel_id=1, replica_groups=mesh['dp'=8,'mp'=4] {'dp','mp'}, use_global_device_ids=true, to_apply=%region_25.26 | all-reduce | flops 3072 | bytes 24576 | tf_op jit(solution)/shard_map/psum | solution.py:225
  380.7 3.7 add_add_fusion.2
  384.4 360.6 %all-reduce.4.cloned.1.call-done = (f32[768,3,192]{0,2,1:T(8,128)}, f32[192,768]{1,0:T(8,128)}, f32[2,768,768]{2,1,0:T(8,128)}, f32[2,768,768]{2,1,0:T(8,128)}) async-done(((f32[768,3,192]{0,2,1:T(8,128)}, f32[192,768]{1,0:T(8,128)}, f32[2,768,768]{2,1,0:T(8,128)}, f32[2,768,768]{2,1,0:T(8,128)}), (f32[768,3,192]{0,2,1:T(8,128)}, f32[192,768]{1,0:T(8,128)}, f32[2,768,768]{2,1,0:T(8,128)}, ...) | async-done | bytes 11796496 | tf_op jit(solution)/shard_map/psum | solution.py:228
  745.0 2.9 copy.95
  748.0 2.1 copy.96
  750.0 2.2 copy.97
  752.2 2.2 copy.98
  (104 shorter events, 1.8 us)
Async XLA Ops:
  7.2 36.8 %copy-start = (bf16[768,3,192]{0,2,1:T(8,128)(2,1)S(1)}, bf16[768,3,192]{0,2,1:T(8,128)(2,1)}, u32[]{:S(2)}) copy-start(bf16[768,3,192]{0,2,1:T(8,128)(2,1)} %param.18) | copy-start | bytes 2654212
  7.2 5.5 copy-start.19
  7.2 5.5 copy-start.20
  7.2 36.8 %all-gather.5.cloned.1.call-start = ((), (), s32[]{:S(2)}) async-start(), calls=%async_computation.4 | async-start | bytes 3932160 | tf_op jit(solution)/shard_map/all_gather | solution.py:55
  12.6 82.2 %reduce-scatter.5.cloned.1.call-start = ((), (), s32[]{:S(2)}) async-start(), calls=%async_computation.5 | async-start | bytes 3932160 | tf_op jit(solution)/shard_map/reduce_scatter | solution.py:90
  47.9 2.5 copy-start.14
  49.2 2.7 copy-start.2
  51.9 2.1 copy-start.16
  53.1 0.9 copy-start.10
  54.0 2.9 copy-start.27
  54.0 15.8 %copy-start.7 = (bf16[2,256,768]{2,1,0:T(8,128)(2,1)S(1)}, bf16[2,256,768]{2,1,0:T(8,128)(2,1)}, u32[]{:S(2)}) copy-start(bf16[2,256,768]{2,1,0:T(8,128)(2,1)} %param.14) | copy-start | bytes 2359300
  56.7 38.1 %copy-start.1 = (bf16[2,256,768]{2,1,0:T(8,128)(2,1)S(1)}, bf16[2,256,768]{2,1,0:T(8,128)(2,1)}, u32[]{:S(2)}) copy-start(bf16[2,256,768]{2,1,0:T(8,128)(2,1)} %param.13) | copy-start | bytes 2359300
  56.8 41.1 %copy-start.17 = (f32[768]{0:T(1024)S(1)}, f32[768]{0:T(1024)}, u32[]{:S(2)}) copy-start(f32[768]{0:T(1024)} %param.24) | copy-start | bytes 9220
  56.8 41.1 %copy-start.21 = (f32[768]{0:T(1024)S(1)}, f32[768]{0:T(1024)}, u32[]{:S(2)}) copy-start(f32[768]{0:T(1024)} %param.25) | copy-start | bytes 9220
  56.8 68.7 %all-gather.9.cloned.1.call-start = ((), (), s32[]{:S(2)}) async-start(), calls=%async_computation.8 | async-start | bytes 3932160 | tf_op jit(solution)/shard_map/all_gather | solution.py:134
  68.4 30.7 %copy-start.28 = (s32[2]{0:T(128)}, s32[2]{0:T(128)S(1)}, u32[]{:S(2)}) copy-start(s32[2]{0:T(128)S(1)} %psum.63) | copy-start | bytes 28
  71.0 85.0 %all-gather.7.cloned.1.call-start = ((), (), s32[]{:S(2)}) async-start(), calls=%async_computation.6 | async-start | bytes 3932160 | tf_op jit(solution)/shard_map/all_gather | solution.py:100
  94.8 3.1 copy-start.3
  99.2 139.1 %reduce-scatter.9.cloned.1.call-start = ((), (), s32[]{:S(2)}) async-start(), calls=%async_computation.9 | async-start | bytes 3932160 | tf_op jit(solution)/shard_map/reduce_scatter | solution.py:168
  156.0 5.1 copy-start.23
  156.0 5.1 copy-start.25
  191.4 4.7 copy-start.29
  200.3 73.6 %all-gather.11.cloned.1.call-start = ((), (), s32[]{:S(2)}) async-start(), calls=%async_computation.10 | async-start | bytes 3932160 | tf_op jit(solution)/shard_map/all_gather | solution.py:174
  238.3 4.1 copy-start.4
  245.3 91.8 %reduce-scatter.11.cloned.1.call-start = ((), (), s32[]{:S(2)}) async-start(), calls=%async_computation.11 | async-start | bytes 3932160 | tf_op jit(solution)/shard_map/reduce_scatter | solution.py:214
  273.9 7.3 slice-start
  277.2 4.1 slice-start.1
  286.5 4.6 copy-start.15
  293.1 1.5 copy-start.5
  299.0 81.7 %reduce-scatter.7.cloned.1.call-start = ((), (), s32[]{:S(2)}) async-start(), calls=%async_computation.7 | async-start | bytes 3932160 | tf_op jit(solution)/shard_map/reduce_scatter | solution.py:120
  299.0 5.1 copy-start.12
  299.0 5.1 copy-start.26
  308.2 436.8 %all-reduce.4.cloned.1.call-start = ((), (), s32[]{:S(2)}) async-start(), calls=%async_computation.12 | async-start | bytes 23592960 | tf_op jit(solution)/shard_map/psum | solution.py:228
  308.5 5.9 copy-start.24
  308.5 5.9 copy-start.30
  314.4 2.9 copy-start.13
  314.4 3.2 copy-start.22
  323.3 4.4 copy-start.9
  323.3 4.4 copy-start.11
  327.7 1.7 copy-start.6
  334.8 2.2 copy-start.18
  745.0 5.0 copy-start.8
  748.0 4.3 slice-start.2
  750.0 2.2 slice-start.3
Sparse Core Ops, SparseCore 0:
  12.7 31.2 all-gather.4
  56.9 37.8 reduce-scatter.4
  96.9 28.4 all-gather.8
  127.5 28.4 all-gather.6
  200.4 37.8 reduce-scatter.8
  245.4 28.5 all-gather.10
  299.1 37.8 reduce-scatter.10
  339.5 38.0 reduce-scatter.6
  382.8 362.1 all-reduce.3
where the time goes:
time: 769 us; the launch traced here: 761 us
  waiting for transfers between devices  533 us (69%)
  matrix products  94.5 us (12%)
  other arithmetic  52.9 us (7%)
  blocking collectives  51.2 us (7%)
  between operations  14.8 us (2%)
  local copies, waits for them, and re-layouts  14.1 us (2%)
    psum x1, waiting for transfers between devices, per_device(): lax.psum((grad_qkv_weight, grad_out_weight, grad_in_weight, grad_down_wei...  361 us
    psum x1, blocking collectives, per_device(): lax.psum((grad_gain_attn, grad_shift_attn, grad_gain_ffn, grad_shift_ffn)...  39.9 us
    reduce_scatter x2, waiting for transfers between devices, per_device(): lax.psum_scatter(total.astype(jnp.bfloat16), 'mp', scatter_dimension=0, t...  38 us
    all_gather x1, waiting for transfers between devices, per_device(): norm_one_full = lax.all_gather(norm_one, 'mp', axis=0, tiled=True)  30.5 us
    all_gather x1, waiting for transfers between devices, per_device(): lax.all_gather(grad_residual.astype(jnp.bfloat16), 'mp', axis=0, tiled=True)  28.4 us
    all_gather x1, waiting for transfers between devices, per_device(): lax.all_gather(grad_output.astype(jnp.bfloat16), 'mp', axis=0, tiled=True)  26 us
    reduce_scatter x1, waiting for transfers between devices, per_device(): lax.psum_scatter(jnp.einsum('rsk,kd->rsd', picked, out_weight, preferred_...  23.8 us
    all_gather x1, waiting for transfers between devices, per_device(): norm_two_full = lax.all_gather(norm_two, 'mp', axis=0, tiled=True)  23 us
  transfers between devices with their start and end apart: 9, of which 8 were waited for; matrix products, arithmetic and copies ran while one was open for 8% of the time, Pallas kernels for 0%

commit v1 on v0

--- a/solution.py
+++ b/solution.py
@@ -225,7 +225,14 @@
     norm_grads = lax.psum(
         (grad_gain_attn, grad_shift_attn, grad_gain_ffn, grad_shift_ffn), ("dp", "mp")
     )
-    summed = lax.psum((grad_qkv_weight, grad_out_weight, grad_in_weight, grad_down_weight), "dp")
+    summed = lax.psum(
+        tuple(
+            g.astype(jnp.bfloat16)
+            for g in (grad_qkv_weight, grad_out_weight, grad_in_weight, grad_down_weight)
+        ),
+        "dp",
+    )
+    summed = tuple(g.astype(jnp.float32) for g in summed)
     return (
         output,
         grad_tokens,

time: 769 us -> 604 us (0.79)
  waiting for transfers between devices: 533 us -> 367 us
  other arithmetic: 52.9 us -> 61.1 us
    psum x1, waiting for transfers between devices: 361 us -> 186 us  [per_device(): lax.psum(tuple((g.astype(jnp.bfloat16) for g in (grad_qkv_weight, grad_ou...]
    reduce_scatter x1, waiting for transfers between devices: 2.21 us -> 29.4 us  [per_device(): lax.psum_scatter(jnp.einsum('rsk,dk->rsd', picked, qkv_flat, preferred_el...]
    all_gather x1, waiting for transfers between devices: 28.4 us -> 10.8 us  [per_device(): lax.all_gather(grad_residual.astype(jnp.bfloat16), 'mp', axis=0, tiled=True)]
    convert_element_type x0 -> x4, other arithmetic: none -> 10 us  [per_device(): summed = tuple((g.astype(jnp.float32) for g in summed))]
  transfers between devices with their start and end apart: 9 -> 9, of which waited for: 8 -> 8; matrix products, arithmetic and copies ran while one was open for 8% -> 10% of each run, Pallas kernels for 0% -> 0%
where the time goes in v1:
time: 604 us; the launch traced here: 596 us
  waiting for transfers between devices  367 us (61%)
  matrix products  91.9 us (15%)
  other arithmetic  61.1 us (10%)
  blocking collectives  51.3 us (8%)
  between operations  14.8 us (2%)
  local copies, waits for them, and re-layouts  8.84 us (1%)
    psum x1, waiting for transfers between devices, per_device(): lax.psum(tuple((g.astype(jnp.bfloat16) for g in (grad_qkv_weight, grad_ou...  186 us
    psum x1, blocking collectives, per_device(): lax.psum((grad_gain_attn, grad_shift_attn, grad_gain_ffn, grad_shift_ffn)...  39.9 us
    reduce_scatter x2, waiting for transfers between devices, per_device(): lax.psum_scatter(total.astype(jnp.bfloat16), 'mp', scatter_dimension=0, t...  38 us
    all_gather x1, waiting for transfers between devices, per_device(): norm_one_full = lax.all_gather(norm_one, 'mp', axis=0, tiled=True)  30.5 us
    reduce_scatter x1, waiting for transfers between devices, per_device(): lax.psum_scatter(jnp.einsum('rsk,dk->rsd', picked, qkv_flat, preferred_el...  29.4 us
    all_gather x1, waiting for transfers between devices, per_device(): lax.all_gather(grad_output.astype(jnp.bfloat16), 'mp', axis=0, tiled=True)  26 us
    reduce_scatter x1, waiting for transfers between devices, per_device(): lax.psum_scatter(jnp.einsum('rsk,kd->rsd', picked, out_weight, preferred_...  23.8 us
    all_gather x1, waiting for transfers between devices, per_device(): norm_two_full = lax.all_gather(norm_two, 'mp', axis=0, tiled=True)  23 us
  transfers between devices with their start and end apart: 9, of which 8 were waited for; matrix products, arithmetic and copies ran while one was open for 10% of the time, Pallas kernels for 0%

profile of v1, /device:TPU:0, one launch (start us, length us, event | category | flops | bytes accessed | tf_op | source)
XLA Modules:
  0.0 596.3 jit_solution(15149717296624991577)
XLA Ops:
  7.3 1.4 convert_reduce_fusion.2
  8.6 1.5 fusion.66
  10.2 2.4 fusion.64
  12.7 0.7 or_and_fusion
  13.4 30.5 %all-gather.5.cloned.1.call-done = bf16[8,256,768]{2,1,0:T(8,128)(2,1)} async-done(((bf16[2,256,768]{2,1,0:T(8,128)(2,1)}), bf16[8,256,768]{2,1,0:T(8,128)(2,1)}) %all-gather.5.cloned.1.call-update) | async-done | bytes 3145744 | tf_op jit(solution)/shard_map/all_gather | solution.py:55
  44.0 3.9 convolution_convert_fusion.2
  47.9 1.3 fusion.133
  49.3 1.1 fusion.6
  50.4 1.5 copy-done.2
  51.9 1.2 fusion.102
  53.1 0.9 copy-done.7
  54.0 2.7 convolution_convert_fusion.1
  57.1 11.4 %psum.63 = s32[2]{0:T(128)S(1)} all-reduce(s32[2]{0:T(128)S(1)} %select_reduce_fusion), channel_id=1, replica_groups=mesh['dp'=8,'mp'=4] {'dp'}, use_global_device_ids=true, to_apply=%region_10.11 | all-reduce | flops 2 | bytes 16 | tf_op jit(solution)/shard_map/psum | solution.py:51
  69.0 0.7 multiply_divide_fusion
  69.8 1.1 fusion.70
  71.0 23.8 %reduce-scatter.5.cloned.1.call-done = bf16[2,256,768]{2,1,0:T(8,128)(2,1)} async-done(((bf16[8,256,768]{2,1,0:T(8,128)(2,1)}), bf16[2,256,768]{2,1,0:T(8,128)(2,1)}) %reduce-scatter.5.cloned.1.call-update) | async-done | bytes 786448 | tf_op jit(solution)/shard_map/reduce_scatter | solution.py:90
  94.8 1.5 fusion.104
  96.3 1.5 multiply_reduce_fusion.1
  97.9 1.3 add_convert_fusion.4
  99.5 26.0 %all-gather.9.cloned.1.call-done = bf16[8,256,768]{2,1,0:T(8,128)(2,1)} async-done(((bf16[2,256,768]{2,1,0:T(8,128)(2,1)}), bf16[8,256,768]{2,1,0:T(8,128)(2,1)}) %all-gather.9.cloned.1.call-update) | async-done | bytes 3145744 | tf_op jit(solution)/shard_map/all_gather | solution.py:134
  125.5 7.5 %fusion.24 = f32[8,256,768]{2,1,0:T(8,128)} fusion(bf16[8,256,768]{2,1,0:T(8,128)(2,1)} %all-gather.9.cloned.1.call-done, bf16[8]{0:T(256)(128)(2,1)S(1)} %get-tuple-element.36, bf16[2,768,768]{2,1,0:T(8,128)(2,1)} %param.21), kind=kOutput, calls=%fused_computation.47 | convolution fusion | flops 2417491968 | bytes 10616848 | tf_op jit(solution)/shard_map/rsd,fd->rsf/dot_general | solution.py:139
  133.0 23.0 %all-gather.7.cloned.1.call-done = bf16[8,256,768]{2,1,0:T(8,128)(2,1)} async-done(((bf16[2,256,768]{2,1,0:T(8,128)(2,1)}), bf16[8,256,768]{2,1,0:T(8,128)(2,1)}) %all-gather.7.cloned.1.call-update) | async-done | bytes 3145744 | tf_op jit(solution)/shard_map/all_gather | solution.py:100
  156.0 5.1 fusion.32
  161.1 4.6 fusion.84
  165.7 15.1 %multiply_convert_fusion.1 = (bf16[8,256,768]{2,1,0:T(8,128)(2,1)}, f32[8,256,768]{2,1,0:T(8,128)S(1)}) fusion(f32[8,256,768]{2,1,0:T(8,128)S(1)} %get-tuple-element.39, u8[256,768]{1,0:T(8,128)(4,1)S(1)} %get-tuple-element.12, u8[256,768]{1,0:T(8,128)(4,1)S(1)} %get-tuple-element.11), kind=kLoop, calls=%fused_computation.13 | loop fusion | flops 110100480 | bytes 16121856 | tf_op jit(solution)/shard_map/convert_element_type | solution.py:109
  180.9 10.6 %add_convert_fusion.1 = bf16[8,256,768]{2,1,0:T(8,128)(2,1)} fusion(f32[8,256,768]{2,1,0:T(8,128)S(1)} %get-tuple-element.30, f32[8,256,768]{2,1,0:T(8,128)} %fusion.24, f32[8,256,768]{2,1,0:T(8,128)S(1)} %get-tuple-element.39, bf16[8,256,768]{2,1,0:T(8,128)(2,1)} %all-gather.9.cloned.1.call-done, bf16[8]{0:T(256)(128)(2,1)S(1)} %get-tuple-element.35, ...), kind=kOutput, calls=%fused_computation.11 | convolution fusion | flops 2441084928 | bytes 26345488 | tf_op jit(solution)/shard_map/rsd,fd->rsf/dot_general | solution.py:139
  191.4 4.7 fusion.13
  196.2 4.1 add_convert_fusion
  200.4 38.0 %reduce-scatter.9.cloned.1.call-done = bf16[2,256,768]{2,1,0:T(8,128)(2,1)} async-done(((bf16[8,256,768]{2,1,0:T(8,128)(2,1)}), bf16[2,256,768]{2,1,0:T(8,128)(2,1)}) %reduce-scatter.9.cloned.1.call-update) | async-done | bytes 786448 | tf_op jit(solution)/shard_map/reduce_scatter | solution.py:168
  238.4 1.9 convert_reduce_fusion.1
  240.2 2.2 fusion.68
  242.4 2.8 fusion.123
  245.6 5.7 fusion.93
  251.3 2.8 fusion.90
  254.2 0.8 copy-done.24
  254.9 2.8 fusion.99
  257.7 2.8 fusion.96
  260.5 2.6 pad_maximum_fusion
  263.1 10.8 %all-gather.11.cloned.1.call-done = bf16[8,256,768]{2,1,0:T(8,128)(2,1)} async-done(((bf16[2,256,768]{2,1,0:T(8,128)(2,1)}), bf16[8,256,768]{2,1,0:T(8,128)(2,1)}) %all-gather.11.cloned.1.call-update) | async-done | bytes 3145744 | tf_op jit(solution)/shard_map/all_gather | solution.py:174
  274.0 3.2 convolution_convert_fusion.3
  277.2 4.9 fusion.87
  282.2 4.1 multiply_reduce_fusion
  286.3 4.5 multiply_convert_fusion
  290.7 1.1 multiply_bitcast_fusion
  291.8 0.7 multiply_bitcast_fusion.1
  293.2 0.9 copy-done.8
  294.1 1.0 copy-done.9
  295.1 1.5 fusion.105
  296.6 1.3 copy-done.23
  297.9 3.0 bitcast_convert_fusion.4
  301.0 1.8 copy.69
  302.8 4.1 convolution_convert_fusion
  307.2 5.3 fusion.17
  312.6 4.1 add_convert_fusion.2
  316.7 185.7 %all-reduce.4.cloned.1.call-done = (bf16[768,3,192]{0,2,1:T(8,128)(2,1)}, bf16[192,768]{1,0:T(8,128)(2,1)}, bf16[2,768,768]{2,1,0:T(8,128)(2,1)}, bf16[2,768,768]{2,1,0:T(8,128)(2,1)}) async-done(((bf16[768,3,192]{0,2,1:T(8,128)(2,1)}, bf16[192,768]{1,0:T(8,128)(2,1)}, bf16[2,768,768]{2,1,0:T(8,128)(2,1)}, bf16[2,768,768]{2,1,0:T(8,128)(2,1)}), (bf16[768,3,192]{0,2,1:T(8,128)(2,1)}, ...) | async-done | bytes 5898256 | tf_op jit(solution)/shard_map/psum | solution.py:228
  502.5 2.0 convert_element_type.152
  504.4 2.5 convert_element_type.150
  507.0 2.8 convert_element_type.153
  509.8 2.7 convert_element_type.154
  512.5 29.4 %reduce-scatter.11.cloned.1.call-done = bf16[2,256,768]{2,1,0:T(8,128)(2,1)} async-done(((bf16[8,256,768]{2,1,0:T(8,128)(2,1)}), bf16[2,256,768]{2,1,0:T(8,128)(2,1)}) %reduce-scatter.11.cloned.1.call-update) | async-done | bytes 786448 | tf_op jit(solution)/shard_map/reduce_scatter | solution.py:214
  541.9 1.7 convert_reduce_fusion
  543.6 2.1 fusion.69
  545.7 39.9 %all-reduce = (f32[768]{0:T(1024)}, f32[768]{0:T(1024)}, f32[768]{0:T(1024)}, f32[768]{0:T(1024)}) all-reduce(f32[768]{0:T(1024)S(1)} %get-tuple-element.15, f32[768]{0:T(1024)S(1)} %get-tuple-element.19, f32[768]{0:T(1024)S(1)} %get-tuple-element.13, f32[768]{0:T(1024)S(1)} %get-tuple-element.17), channel_id=1, replica_groups=mesh['dp'=8,'mp'=4] {'dp','mp'}, use_global_device_ids=true, to_apply=%region_25.26 | all-reduce | flops 3072 | bytes 24576 | tf_op jit(solution)/shard_map/psum | solution.py:225
  585.6 3.7 add_add_fusion.2
  (103 shorter events, 3.1 us)
Async XLA Ops:
  7.2 36.8 %copy-start = (bf16[768,3,192]{0,2,1:T(8,128)(2,1)S(1)}, bf16[768,3,192]{0,2,1:T(8,128)(2,1)}, u32[]{:S(2)}) copy-start(bf16[768,3,192]{0,2,1:T(8,128)(2,1)} %param.18) | copy-start | bytes 2654212
  7.2 5.5 copy-start.20
  7.2 5.5 copy-start.21
  7.2 36.8 %all-gather.5.cloned.1.call-start = ((), (), s32[]{:S(2)}) async-start(), calls=%async_computation.4 | async-start | bytes 3932160 | tf_op jit(solution)/shard_map/all_gather | solution.py:55
  12.6 82.2 %reduce-scatter.5.cloned.1.call-start = ((), (), s32[]{:S(2)}) async-start(), calls=%async_computation.5 | async-start | bytes 3932160 | tf_op jit(solution)/shard_map/reduce_scatter | solution.py:90
  47.9 2.5 copy-start.13
  49.2 2.7 copy-start.2
  51.9 2.1 copy-start.17
  53.1 0.9 copy-start.7
  54.0 2.9 copy-start.29
  54.0 15.8 %copy-start.6 = (bf16[2,256,768]{2,1,0:T(8,128)(2,1)S(1)}, bf16[2,256,768]{2,1,0:T(8,128)(2,1)}, u32[]{:S(2)}) copy-start(bf16[2,256,768]{2,1,0:T(8,128)(2,1)} %param.14) | copy-start | bytes 2359300
  56.7 38.1 %copy-start.1 = (bf16[2,256,768]{2,1,0:T(8,128)(2,1)S(1)}, bf16[2,256,768]{2,1,0:T(8,128)(2,1)}, u32[]{:S(2)}) copy-start(bf16[2,256,768]{2,1,0:T(8,128)(2,1)} %param.13) | copy-start | bytes 2359300
  56.8 41.1 %copy-start.18 = (f32[768]{0:T(1024)S(1)}, f32[768]{0:T(1024)}, u32[]{:S(2)}) copy-start(f32[768]{0:T(1024)} %param.24) | copy-start | bytes 9220
  56.8 41.1 %copy-start.22 = (f32[768]{0:T(1024)S(1)}, f32[768]{0:T(1024)}, u32[]{:S(2)}) copy-start(f32[768]{0:T(1024)} %param.25) | copy-start | bytes 9220
  56.8 68.7 %all-gather.9.cloned.1.call-start = ((), (), s32[]{:S(2)}) async-start(), calls=%async_computation.8 | async-start | bytes 3932160 | tf_op jit(solution)/shard_map/all_gather | solution.py:134
  68.4 30.7 %copy-start.30 = (s32[2]{0:T(128)}, s32[2]{0:T(128)S(1)}, u32[]{:S(2)}) copy-start(s32[2]{0:T(128)S(1)} %psum.63) | copy-start | bytes 28
  71.0 85.0 %all-gather.7.cloned.1.call-start = ((), (), s32[]{:S(2)}) async-start(), calls=%async_computation.6 | async-start | bytes 3932160 | tf_op jit(solution)/shard_map/all_gather | solution.py:100
  94.8 3.1 copy-start.3
  99.2 139.2 %reduce-scatter.9.cloned.1.call-start = ((), (), s32[]{:S(2)}) async-start(), calls=%async_computation.9 | async-start | bytes 3932160 | tf_op jit(solution)/shard_map/reduce_scatter | solution.py:168
  156.0 5.1 copy-start.25
  156.0 5.1 copy-start.27
  191.4 4.7 copy-start.31
  200.3 73.6 %all-gather.11.cloned.1.call-start = ((), (), s32[]{:S(2)}) async-start(), calls=%async_computation.10 | async-start | bytes 3932160 | tf_op jit(solution)/shard_map/all_gather | solution.py:174
  238.4 4.1 copy-start.4
  245.3 257.2 %all-reduce.4.cloned.1.call-start = ((), (), s32[]{:S(2)}) async-start(), calls=%async_computation.12 | async-start | bytes 11796480 | tf_op jit(solution)/shard_map/psum | solution.py:228
  245.5 5.8 copy-start.26
  245.5 5.8 copy-start.32
  251.3 2.8 copy-start.10
  251.3 3.6 copy-start.24
  274.0 8.2 %slice-start = ((s8[6291456]{0:T(1024)(128)(4,1)}), s8[4194304]{0:T(1024)(128)(4,1)S(1)}, s32[]{:S(2)}) async-start(s8[6291456]{0:T(1024)(128)(4,1)} %bitcast.141), calls=%async_computation.13 | async-start | bytes 8388608
  277.2 5.0 slice-start.1
  277.2 4.9 copy-start.14
  291.8 1.1 copy-start.12
  293.0 1.1 copy-start.8
  293.0 2.1 copy-start.9
  295.1 5.8 copy-start.5
  295.1 2.8 copy-start.23
  300.9 241.0 %reduce-scatter.11.cloned.1.call-start = ((), (), s32[]{:S(2)}) async-start(), calls=%async_computation.11 | async-start | bytes 3932160 | tf_op jit(solution)/shard_map/reduce_scatter | solution.py:214
  306.9 278.7 %reduce-scatter.7.cloned.1.call-start = ((), (), s32[]{:S(2)}) async-start(), calls=%async_computation.7 | async-start | bytes 3932160 | tf_op jit(solution)/shard_map/reduce_scatter | solution.py:120
  307.2 5.4 copy-start.11
  307.2 5.4 copy-start.28
  502.5 4.5 copy-start.16
  507.0 2.8 copy-start.15
  509.8 32.1 %copy-start.19 = (f32[768]{0:T(1024)S(1)}, f32[768]{0:T(1024)}, u32[]{:S(2)}) copy-start(f32[768]{0:T(1024)} %param.22) | copy-start | bytes 9220
Sparse Core Ops, SparseCore 0:
  12.7 31.2 all-gather.4
  56.9 37.8 reduce-scatter.4
  96.9 28.4 all-gather.8
  127.5 28.4 all-gather.6
  200.4 37.8 reduce-scatter.8
  245.4 28.4 all-gather.10
  301.1 201.3 all-reduce.3
  505.0 36.8 reduce-scatter.10
  544.5 38.0 reduce-scatter.6

commit v2 on v0

--- a/solution.py
+++ b/solution.py
@@ -19,6 +19,60 @@
 
 def gelu_exact(values):
     return jax.nn.gelu(values, approximate=False)
+
+
+def xor_pairs(size, bit):
+    return [(i, i ^ bit) for i in range(size)]
+
+
+def gather_rows_mp(values):
+    if lax.axis_size("mp") != 4:
+        return lax.all_gather(values, "mp", axis=0, tiled=True)
+    index = lax.axis_index("mp")
+    chip_y = index // 2
+    core = index % 2
+    other_y = lax.ppermute(values, "mp", xor_pairs(4, 2))
+    pair = jnp.where(
+        chip_y == 0, jnp.stack([values, other_y]), jnp.stack([other_y, values])
+    )
+    other_core = lax.ppermute(pair, "mp", xor_pairs(4, 1))
+    quad = jnp.where(
+        core == 0, jnp.stack([pair, other_core], axis=1), jnp.stack([other_core, pair], axis=1)
+    )
+    return quad.reshape((-1,) + values.shape[1:])
+
+
+def scatter_rows_mp(partial):
+    if lax.axis_size("mp") != 4:
+        return lax.psum_scatter(
+            partial.astype(jnp.bfloat16), "mp", scatter_dimension=0, tiled=True
+        ).astype(jnp.float32)
+    index = lax.axis_index("mp")
+    chip_y = index // 2
+    core = index % 2
+    rows = partial.shape[0] // 4
+    blocks = partial.reshape((2, 2, rows) + partial.shape[1:])
+    keep = lax.dynamic_index_in_dim(blocks, core, axis=1, keepdims=False)
+    send = lax.dynamic_index_in_dim(blocks, 1 - core, axis=1, keepdims=False)
+    got = lax.ppermute(send.astype(jnp.bfloat16), "mp", xor_pairs(4, 1))
+    chip_sum = keep + got.astype(jnp.float32)
+    keep_y = lax.dynamic_index_in_dim(chip_sum, chip_y, axis=0, keepdims=False)
+    send_y = lax.dynamic_index_in_dim(chip_sum, 1 - chip_y, axis=0, keepdims=False)
+    got_y = lax.ppermute(send_y.astype(jnp.bfloat16), "mp", xor_pairs(4, 2))
+    return keep_y + got_y.astype(jnp.float32)
+
+
+def butterfly_sum(values, axis):
+    size = lax.axis_size(axis)
+    if size & (size - 1):
+        return lax.psum(values, axis)
+    bit = 1
+    while bit < size:
+        values = jax.tree.map(
+            lambda v: v + lax.ppermute(v, axis, xor_pairs(size, bit)), values
+        )
+        bit *= 2
+    return values
 
 
 def select_rows(values, hot_column):
@@ -48,11 +102,11 @@
     expert_hot = expert_ids[:, None] == jnp.arange(experts)[None, :]
     row_live = jnp.sum(live_mask, axis=1)
     local_counts = jnp.sum(jnp.where(expert_hot, row_live[:, None], 0), axis=0)
-    counts = lax.psum(local_counts, "dp")
+    counts = butterfly_sum(local_counts, "dp")
     hot_matrix = expert_hot.astype(jnp.bfloat16)
     token_float = tokens.astype(jnp.float32)
     norm_one = layer_norm(token_float, gain_attn, shift_attn).astype(jnp.bfloat16)
-    norm_one_full = lax.all_gather(norm_one, "mp", axis=0, tiled=True)
+    norm_one_full = gather_rows_mp(norm_one)
     qkv_flat = qkv_weight.reshape(model_width, -1)
     qkv_all = jnp.einsum(
         "rsd,dk->rsk", norm_one_full, qkv_flat, preferred_element_type=jnp.float32
@@ -87,17 +141,12 @@
     )
     head_mix = head_mix.reshape(group_rows, slots, heads_local * HD).astype(jnp.bfloat16)
     picked = head_mix
-    attn_local = lax.psum_scatter(
-        jnp.einsum("rsk,kd->rsd", picked, out_weight, preferred_element_type=jnp.float32).astype(
-            jnp.bfloat16
-        ),
-        "mp",
-        scatter_dimension=0,
-        tiled=True,
-    ).astype(jnp.float32)
+    attn_local = scatter_rows_mp(
+        jnp.einsum("rsk,kd->rsd", picked, out_weight, preferred_element_type=jnp.float32)
+    )
     residual = token_float + attn_local
     norm_two = layer_norm(residual, gain_ffn, shift_ffn).astype(jnp.bfloat16)
-    norm_two_full = lax.all_gather(norm_two, "mp", axis=0, tiled=True)
+    norm_two_full = gather_rows_mp(norm_two)
     upward = jnp.zeros((group_rows, slots, in_weight.shape[2]), jnp.float32)
     for expert in range(experts):
         upward = upward + jnp.einsum(
@@ -117,9 +166,7 @@
             down_weight[ffn_expert],
             preferred_element_type=jnp.float32,
         )
-    ffn_local = lax.psum_scatter(
-        total.astype(jnp.bfloat16), "mp", scatter_dimension=0, tiled=True
-    ).astype(jnp.float32)
+    ffn_local = scatter_rows_mp(total)
     output = (residual + ffn_local).astype(jnp.bfloat16)
     count_float = counts.astype(jnp.float32)
     loss_weight = jnp.sum(count_float) / (experts * count_float)
@@ -131,7 +178,7 @@
         * live_local[:, :, None].astype(jnp.float32)
         * row_weight[:, None, None]
     )
-    grad_ffn_full = lax.all_gather(grad_output.astype(jnp.bfloat16), "mp", axis=0, tiled=True)
+    grad_ffn_full = gather_rows_mp(grad_output.astype(jnp.bfloat16))
     grad_act = jnp.zeros(upward.shape, jnp.float32)
     down_list = []
     for expert in range(experts):
@@ -155,6 +202,7 @@
             )
         )
     grad_in_weight = jnp.stack(in_list, axis=0)
+    ffn_grads = (grad_in_weight.astype(jnp.bfloat16), grad_down_weight.astype(jnp.bfloat16))
     picked = grad_up
     hot_picked = hot_matrix
     total = jnp.zeros((local_rows * lax.axis_size("mp"), slots, model_width), jnp.float32)
@@ -165,13 +213,13 @@
             in_weight[expert],
             preferred_element_type=jnp.float32,
         )
-    grad_norm_two = lax.psum_scatter(
-        total.astype(jnp.bfloat16), "mp", scatter_dimension=0, tiled=True
-    ).astype(jnp.float32)
+    grad_norm_two = scatter_rows_mp(total)
     second_back = jax.vjp(layer_norm, residual, gain_ffn, shift_ffn)[1]
     grad_from_second, grad_gain_ffn, grad_shift_ffn = second_back(grad_norm_two)
     grad_residual = grad_output + grad_from_second
-    grad_attn_full = lax.all_gather(grad_residual.astype(jnp.bfloat16), "mp", axis=0, tiled=True)
+    ffn_grads, grad_residual = lax.optimization_barrier((ffn_grads, grad_residual))
+    ffn_summed = lax.psum(ffn_grads, "dp")
+    grad_attn_full = gather_rows_mp(grad_residual.astype(jnp.bfloat16))
     grad_out_weight = jnp.einsum(
         "rsk,rsd->kd", head_mix, grad_attn_full, preferred_element_type=jnp.float32
     )
@@ -211,21 +259,23 @@
     )
     grad_qkv_weight = grad_qkv_weight.reshape(qkv_weight.shape)
     picked = grad_qkv
-    grad_norm_one = lax.psum_scatter(
-        jnp.einsum("rsk,dk->rsd", picked, qkv_flat, preferred_element_type=jnp.float32).astype(
-            jnp.bfloat16
-        ),
-        "mp",
-        scatter_dimension=0,
-        tiled=True,
-    ).astype(jnp.float32)
+    grad_norm_one = scatter_rows_mp(
+        jnp.einsum("rsk,dk->rsd", picked, qkv_flat, preferred_element_type=jnp.float32)
+    )
     first_back = jax.vjp(layer_norm, token_float, gain_attn, shift_attn)[1]
     grad_from_first, grad_gain_attn, grad_shift_attn = first_back(grad_norm_one)
     grad_tokens = grad_residual + grad_from_first
-    norm_grads = lax.psum(
-        (grad_gain_attn, grad_shift_attn, grad_gain_ffn, grad_shift_ffn), ("dp", "mp")
-    )
-    summed = lax.psum((grad_qkv_weight, grad_out_weight, grad_in_weight, grad_down_weight), "dp")
+    norm_grads = butterfly_sum(
+        butterfly_sum(
+            jnp.stack([grad_gain_attn, grad_shift_attn, grad_gain_ffn, grad_shift_ffn]), "mp"
+        ),
+        "dp",
+    )
+    attn_grads, ffn_summed = lax.optimization_barrier(
+        ((grad_qkv_weight.astype(jnp.bfloat16), grad_out_weight.astype(jnp.bfloat16)), ffn_summed)
+    )
+    attn_summed = lax.psum(attn_grads, "dp")
+    summed = tuple(g.astype(jnp.float32) for g in attn_summed + ffn_summed)
     return (
         output,
         grad_tokens,

time: 769 us -> 538 us (0.70)
  waiting for transfers between devices: 533 us -> 310 us
  blocking collectives: 51.2 us -> 0 us
  other arithmetic: 52.9 us -> 82.4 us
  starting transfers between devices: 0.97 us -> 25 us
  matrix products: 94.5 us -> 80.8 us
    psum x1 -> x2, waiting for transfers between devices: 361 us -> 175 us  [the longest x1 113 us: per_device(): ffn_summed = lax.psum(ffn_grads, 'dp')]
    ppermute x0 -> x24, waiting for transfers between devices: none -> 135 us  [the longest x4 60 us: gather_rows_mp(): other_y = lax.ppermute(values, 'mp', xor_pairs(4, 2))]
    all_gather x4 -> x0, waiting for transfers between devices: 108 us -> none  [the longest x1 30.5 us: per_device(): norm_one_full = lax.all_gather(norm_one, 'mp', axis=0, tiled=True)]
    reduce_scatter x4 -> x0, waiting for transfers between devices: 64 us -> none  [the longest x2 38 us: per_device(): lax.psum_scatter(total.astype(jnp.bfloat16), 'mp', scatter_dimension=0, t...]
    psum x2 -> x0, blocking collectives: 51.2 us -> none  [the longest x1 39.9 us: per_device(): lax.psum((grad_gain_attn, grad_shift_attn, grad_gain_ffn, grad_shift_ffn)...]
    ppermute x0 -> x24, starting transfers between devices: none -> 25 us  [the longest x8 11.3 us: butterfly_sum(): lax.ppermute(v, axis, xor_pairs(size, bit))]
    select_n x0 -> x10, other arithmetic: none -> 13.7 us  [the longest x8 8.07 us: gather_rows_mp(): jnp.where(chip_y == 0, jnp.stack([values, other_y]), jnp.stack([other_y,...]
    mul x0 -> x3, other arithmetic: none -> 9.37 us  [select_rows(): return values * hot_column[:, None, None]]
  transfers between devices with their start and end apart: 9 -> 26, of which waited for: 8 -> 18; matrix products, arithmetic and copies ran while one was open for 8% -> 17% of each run, Pallas kernels for 0% -> 0%
where the time goes in v2:
time: 538 us; the launch traced here: 535 us
  waiting for transfers between devices  310 us (58%)
  other arithmetic  82.4 us (15%)
  matrix products  80.8 us (15%)
  starting transfers between devices  25 us (5%)
  local copies, waits for them, and re-layouts  20.8 us (4%)
  between operations  15.4 us (3%)
    psum x1, waiting for transfers between devices, per_device(): ffn_summed = lax.psum(ffn_grads, 'dp')  113 us
    psum x1, waiting for transfers between devices, per_device(): attn_summed = lax.psum(attn_grads, 'dp')  62.5 us
    ppermute x4, waiting for transfers between devices, gather_rows_mp(): other_y = lax.ppermute(values, 'mp', xor_pairs(4, 2))  60 us
    ppermute x4, waiting for transfers between devices, scatter_rows_mp(): got_y = lax.ppermute(send_y.astype(jnp.bfloat16), 'mp', xor_pairs(4, 2))  57.4 us
    convert_element_type x1, other arithmetic, per_device(): activated = gelu_exact(upward).astype(jnp.bfloat16)  15 us
    dot_general x2, matrix products, per_device(): jnp.einsum('rsd,fd->rsf', masked_grad, down_weight[expert], preferred_ele...  13.4 us
    unnamed x110, local copies, waits for them, and re-layouts  13.2 us
    ppermute x8, starting transfers between devices, butterfly_sum(): lax.ppermute(v, axis, xor_pairs(size, bit))  11.3 us
  transfers between devices with their start and end apart: 26, of which 18 were waited for; matrix products, arithmetic and copies ran while one was open for 17% of the time, Pallas kernels for 0%

profile of v2, /device:TPU:0, one launch (start us, length us, event | category | flops | bytes accessed | tf_op | source)
XLA Modules:
  0.0 534.6 jit_solution(11677835811281384661)
XLA Ops:
  12.3 3.1 collective-permute-start
  15.8 17.2 %collective-permute-done = bf16[2,256,768]{2,1,0:T(8,128)(2,1)S(1)} collective-permute-done((bf16[2,256,768]{2,1,0:T(8,128)(2,1)S(1)}, bf16[2,256,768]{2,1,0:T(8,128)(2,1)S(1)}, u32[]{:S(2)}, u32[]{:S(2)}) %collective-permute-start) | collective-permute-done | bytes 786464 | tf_op jit(solution)/shard_map/ppermute | solution.py:34
  35.7 2.3 collective-permute-done.1
  38.1 2.6 maximum_select_fusion
  40.9 2.0 convolution_convert_fusion
  49.2 2.6 copy-done.5
  52.6 1.8 collective-permute-start.8
  54.4 1.8 collective-permute-done.8
  56.2 1.8 collective-permute-start.9
  58.0 1.8 collective-permute-done.9
  59.8 2.8 collective-permute-start.10
  62.6 2.7 bitcast_add_fusion.3
  65.4 1.6 collective-permute-start.3
  69.2 16.7 %collective-permute-done.3 = bf16[2,256,768]{2,1,0:T(8,128)(2,1)S(1)} collective-permute-done((bf16[2,256,768]{2,1,0:T(8,128)(2,1)S(1)}, bf16[2,256,768]{2,1,0:T(8,128)(2,1)S(1)}, u32[]{:S(2)}, u32[]{:S(2)}) %collective-permute-start.3) | collective-permute-done | bytes 786464 | tf_op jit(solution)/shard_map/ppermute | solution.py:61
  86.9 1.6 collective-permute-start.4
  88.7 14.0 %collective-permute-done.11 = bf16[2,256,768]{2,1,0:T(8,128)(2,1)S(1)} collective-permute-done((bf16[2,256,768]{2,1,0:T(8,128)(2,1)S(1)}, bf16[2,256,768]{2,1,0:T(8,128)(2,1)S(1)}, u32[]{:S(2)}, u32[]{:S(2)}) %collective-permute-start.11) | collective-permute-done | bytes 786464 | tf_op jit(solution)/shard_map/ppermute | solution.py:34
  104.4 11.8 %collective-permute-done.4 = bf16[2,256,768]{2,1,0:T(8,128)(2,1)S(1)} collective-permute-done((bf16[2,256,768]{2,1,0:T(8,128)(2,1)S(1)}, bf16[2,256,768]{2,1,0:T(8,128)(2,1)S(1)}, u32[]{:S(2)}, u32[]{:S(2)}) %collective-permute-start.4) | collective-permute-done | bytes 786464 | tf_op jit(solution)/shard_map/ppermute | solution.py:34
  119.2 1.7 maximum_select_fusion.7
  121.6 6.2 %broadcast_multiply_fusion = (bf16[2,2,2,256,768]{4,3,2,0,1:T(8,128)(2,1)S(1)}, bf16[2,2,2,256,768]{4,3,2,0,1:T(8,128)(2,1)S(1)}, bf16[2,2,2,256,768]{4,3,2,0,1:T(8,128)(2,1)}, bf16[2,2,2,256,768]{4,3,2,0,1:T(8,128)(2,1)S(1)}) fusion(bf16[2,2,2]{2,0,1:T(2,128)(2,1)S(1)} %copy.51, bf16[2,1,2,256,768]{4,3,2,0,1:T(8,128)(2,1)S(1)} %maximum_select_fusion.7, ...), kind=kLoop, calls=%fused_computation.122 | loop fusion | flops 12582912 | bytes 18874384 | tf_op jit(solution)/shard_map/mul | solution.py:79
  128.9 1.6 copy-done.8
  131.0 1.9 copy.56
  133.8 4.5 fusion.69
  138.3 6.3 %fusion.51 = (u8[256,768]{1,0:T(8,128)(4,1)S(1)}, u8[256,768]{1,0:T(8,128)(4,1)S(1)}, f32[8,256,768]{2,1,0:T(8,128)S(1)}) fusion(f32[8,256,768]{2,1,0:T(8,128)} %fusion.69, bf16[8,256,768]{2,1,0:T(8,128)(2,1)S(1)} %bitcast.282, bf16[2,768,768]{2,1,0:T(8,128)(2,1)S(1)} %copy-done.46), kind=kOutput, calls=%fused_computation.130 | convolution fusion | flops 2437545984 | bytes 17301504 | tf_op jit(solution)/shard_map/rsd,df->rsf/dot_general | solution.py:152
  144.7 4.6 fusion.63
  149.2 15.0 %multiply_convert_fusion.1 = (bf16[8,256,768]{2,1,0:T(8,128)(2,1)}, f32[8,256,768]{2,1,0:T(8,128)}) fusion(f32[8,256,768]{2,1,0:T(8,128)S(1)} %get-tuple-element.77, u8[256,768]{1,0:T(8,128)(4,1)S(1)} %get-tuple-element.26, u8[256,768]{1,0:T(8,128)(4,1)S(1)} %get-tuple-element.25), kind=kLoop, calls=%fused_computation.11 | loop fusion | flops 110100480 | bytes 16121856 | tf_op jit(solution)/shard_map/convert_element_type | solution.py:158
  164.2 8.9 %add_convert_fusion = bf16[8,256,768]{2,1,0:T(8,128)(2,1)} fusion(f32[8,256,768]{2,1,0:T(8,128)} %get-tuple-element.52, f32[8,256,768]{2,1,0:T(8,128)} %fusion.63, f32[8,256,768]{2,1,0:T(8,128)S(1)} %get-tuple-element.77, bf16[8,256,768]{2,1,0:T(8,128)(2,1)S(1)} %bitcast.281, bf16[2,768,768]{2,1,0:T(8,128)(2,1)} %param.21), kind=kOutput, calls=%fused_computation.10 | convolution fusion | flops 2439512064 | bytes 26345472 | tf_op jit(solution)/shard_map/rsd,fd->rsf/dot_general | solution.py:186
  173.1 5.0 fusion.11
  178.2 2.8 fusion.27
  182.9 4.6 fusion.15
  187.5 4.8 fusion.24
  194.3 2.7 bitcast_multiply_fusion.3
  197.0 5.7 %fusion.56 = bf16[1,768,768]{2,1,0:T(8,128)(2,1)S(1)} fusion(bf16[8,256,768]{2,1,0:T(8,128)(2,1)} %get-tuple-element.60, bf16[8,256,768]{2,1,0:T(8,128)(2,1)} %add_convert_fusion), kind=kOutput, calls=%fused_computation.133 | convolution fusion | flops 2416508928 | bytes 7471104 | tf_op jit(solution)/shard_map/rsd,rsf->df/dot_general | solution.py:197
  202.7 2.8 fusion.55
  205.5 2.8 fusion.58
  208.3 2.7 fusion.57
  214.0 1.6 pad_maximum_fusion
  215.6 1.6 pad_maximum_fusion.1
  217.2 2.8 bitcast_add_fusion.1
  220.7 12.5 %collective-permute-done.14 = bf16[2,256,768]{2,1,0:T(8,128)(2,1)} collective-permute-done((bf16[2,256,768]{2,1,0:T(8,128)(2,1)}, bf16[2,256,768]{2,1,0:T(8,128)(2,1)}, u32[]{:S(2)}, u32[]{:S(2)}) %collective-permute-start.14) | collective-permute-done | bytes 786464 | tf_op jit(solution)/shard_map/ppermute | solution.py:61
  233.2 1.6 multiply_reduce_fusion.2
  235.9 13.1 %collective-permute-done.7 = bf16[2,256,768]{2,1,0:T(8,128)(2,1)S(1)} collective-permute-done((bf16[2,256,768]{2,1,0:T(8,128)(2,1)S(1)}, bf16[2,256,768]{2,1,0:T(8,128)(2,1)S(1)}, u32[]{:S(2)}, u32[]{:S(2)}) %collective-permute-start.7) | collective-permute-done | bytes 786464 | tf_op jit(solution)/shard_map/ppermute | solution.py:61
  249.0 1.6 add_add_fusion.3
  250.8 1.6 collective-permute-start.15
  252.4 17.1 %collective-permute-done.15 = bf16[2,256,768]{2,1,0:T(8,128)(2,1)S(1)} collective-permute-done((bf16[2,256,768]{2,1,0:T(8,128)(2,1)S(1)}, bf16[2,256,768]{2,1,0:T(8,128)(2,1)S(1)}, u32[]{:S(2)}, u32[]{:S(2)}) %collective-permute-start.15) | collective-permute-done | bytes 786464 | tf_op jit(solution)/shard_map/ppermute | solution.py:34
  274.6 3.1 maximum_select_fusion.3
  280.1 2.0 fusion.52
  282.1 5.3 multiply_reduce_fusion
  287.4 4.5 multiply_convert_fusion
  291.9 2.2 multiply_bitcast_fusion
  294.1 1.9 multiply_bitcast_fusion.1
  296.4 2.7 fusion.99
  299.5 3.2 collective-permute-done.17
  303.2 1.6 collective-permute-start.18
  304.8 3.0 bitcast_convert_fusion.7
  307.8 15.1 %collective-permute-done.18 = bf16[2,256,768]{2,1,0:T(8,128)(2,1)S(1)} collective-permute-done((bf16[2,256,768]{2,1,0:T(8,128)(2,1)S(1)}, bf16[2,256,768]{2,1,0:T(8,128)(2,1)S(1)}, u32[]{:S(2)}, u32[]{:S(2)}) %collective-permute-start.18) | collective-permute-done | bytes 786464 | tf_op jit(solution)/shard_map/ppermute | solution.py:61
  327.3 112.7 %all-reduce.7.cloned.1.call-done = (bf16[2,768,768]{2,1,0:T(8,128)(2,1)}, bf16[2,768,768]{2,1,0:T(8,128)(2,1)}) async-done(((bf16[2,768,768]{2,1,0:T(8,128)(2,1)}, bf16[2,768,768]{2,1,0:T(8,128)(2,1)}), (bf16[2,768,768]{2,1,0:T(8,128)(2,1)}, bf16[2,768,768]{2,1,0:T(8,128)(2,1)})) %all-reduce.7.cloned.1.call-update) | async-done | bytes 4718608 | tf_op jit(solution)/shard_map/psum | solution.py:221
  441.6 2.2 collective-permute-done.20
  445.4 4.2 convert_element_type.227
  449.6 2.5 convert_element_type.228
  452.3 3.8 collective-permute-done.22
  456.0 1.8 collective-permute-start.23
  457.8 1.7 add_add_fusion.2
  461.6 62.5 %all-reduce.5.cloned.1.call-done = (bf16[768,3,192]{0,2,1:T(8,128)(2,1)}, bf16[192,768]{1,0:T(8,128)(2,1)}) async-done(((bf16[768,3,192]{0,2,1:T(8,128)(2,1)}, bf16[192,768]{1,0:T(8,128)(2,1)}), (bf16[768,3,192]{0,2,1:T(8,128)(2,1)}, bf16[192,768]{1,0:T(8,128)(2,1)})) %all-reduce.5.cloned.1.call-update) | async-done | bytes 1179664 | tf_op jit(solution)/shard_map/psum | solution.py:277
  524.1 2.6 convert_element_type.225
  (228 shorter events, 54.6 us)
Async XLA Ops:
  7.2 33.7 %copy-start = (bf16[768,3,192]{0,2,1:T(8,128)(2,1)S(1)}, bf16[768,3,192]{0,2,1:T(8,128)(2,1)}, u32[]{:S(2)}) copy-start(bf16[768,3,192]{0,2,1:T(8,128)(2,1)} %param.18) | copy-start | bytes 2654212
  7.2 8.2 %copy-start.2 = (bf16[2,256,768]{2,1,0:T(8,128)(2,1)S(1)}, bf16[2,256,768]{2,1,0:T(8,128)(2,1)}, u32[]{:S(2)}) copy-start(bf16[2,256,768]{2,1,0:T(8,128)(2,1)} %param.13) | copy-start | bytes 2359300
  7.2 8.2 %copy-start.40 = (f32[768]{0:T(1024)S(1)}, f32[768]{0:T(1024)}, u32[]{:S(2)}) copy-start(f32[768]{0:T(1024)} %param.23) | copy-start | bytes 9220
  7.2 8.2 %copy-start.32 = (f32[768]{0:T(1024)S(1)}, f32[768]{0:T(1024)}, u32[]{:S(2)}) copy-start(f32[768]{0:T(1024)} %param.22) | copy-start | bytes 9220
  7.2 432.8 %all-reduce.7.cloned.1.call-start = ((), (), s32[]{:S(2)}) async-start(), calls=%async_computation.1 | async-start | bytes 9437184 | tf_op jit(solution)/shard_map/psum | solution.py:221
  8.7 26.4 %copy-start.35 = (f32[2,256]{1,0:T(2,128)}, f32[2,256]{1,0:T(2,128)S(1)}, u32[]{:S(2)}) copy-start(f32[2,256]{1,0:T(2,128)S(1)} %broadcast_multiply_fusion.5) | copy-start | bytes 6148
  10.8 24.3 %copy-start.37 = (f32[2,256]{1,0:T(2,128)}, f32[2,256]{1,0:T(2,128)S(1)}, u32[]{:S(2)}) copy-start(f32[2,256]{1,0:T(2,128)S(1)} %fusion.91) | copy-start | bytes 6148
  12.3 20.6 %collective-permute-start = (bf16[2,256,768]{2,1,0:T(8,128)(2,1)S(1)}, bf16[2,256,768]{2,1,0:T(8,128)(2,1)S(1)}, u32[]{:S(2)}, u32[]{:S(2)}) collective-permute-start(bf16[2,256,768]{2,1,0:T(8,128)(2,1)S(1)} %fusion.33), channel_id=1, source_target_pairs={{0,2},{1,3},{2,0},{3,1},{4,6},{5,7},{6,4},{7,5},{8,10},{9,11},{10,... | collective-permute-start | bytes 2359304 | tf_op jit(solution)/shard_map/ppermute | solution.py:34
  15.4 19.0 %copy-start.39 = (s32[8,256]{1,0:T(8,128)S(1)}, s32[8,256]{1,0:T(8,128)}, u32[]{:S(2)}) copy-start(s32[8,256]{1,0:T(8,128)} %param.16) | copy-start | bytes 24580
  15.4 19.0 %copy-start.42 = (s32[8,256]{1,0:T(8,128)S(1)}, s32[8,256]{1,0:T(8,128)}, u32[]{:S(2)}) copy-start(s32[8,256]{1,0:T(8,128)} %param.15) | copy-start | bytes 24580
  34.3 3.8 collective-permute-start.1
  40.8 2.1 copy-start.16
  42.9 2.5 copy-start.27
  44.3 2.7 copy-start.1
  49.2 2.6 copy-start.5
  52.0 10.6 %collective-permute-start.2 = (bf16[2,2,256,768]{3,2,1,0:T(8,128)(2,1)S(1)}, bf16[2,2,256,768]{3,2,1,0:T(8,128)(2,1)}, u32[]{:S(2)}, u32[]{:S(2)}) collective-permute-start(bf16[2,2,256,768]{3,2,1,0:T(8,128)(2,1)S(1)} %fusion.37), channel_id=1, source_target_pairs={{0,1},{1,0},{2,3},{3,2},{4,5},{5,4},{6,7},{7,6},{8,9},{9,8},{10,11... | collective-permute-start | bytes 4718600 | tf_op jit(solution)/shard_map/ppermute | solution.py:57
  52.6 3.6 collective-permute-start.8
  56.2 3.6 collective-permute-start.9
  59.8 8.5 %copy-start.9 = (bf16[2,256,768]{2,1,0:T(8,128)(2,1)S(1)}, bf16[2,256,768]{2,1,0:T(8,128)(2,1)}, u32[]{:S(2)}) copy-start(bf16[2,256,768]{2,1,0:T(8,128)(2,1)} %param.14) | copy-start | bytes 2359300
  59.8 7.2 %collective-permute-start.10 = (s32[2]{0:T(128)S(1)}, s32[2]{0:T(128)S(1)}, u32[]{:S(2)}, u32[]{:S(2)}) collective-permute-start(s32[2]{0:T(128)S(1)} %add.191), channel_id=1, source_target_pairs={{0,16},{4,20},{8,24},{12,28},{16,0},{20,4},{24,8},{28,12},{1,17},{... | collective-permute-start | bytes 32 | tf_op jit(solution)/shard_map/ppermute | solution.py:72
  65.4 20.5 %collective-permute-start.3 = (bf16[2,256,768]{2,1,0:T(8,128)(2,1)S(1)}, bf16[2,256,768]{2,1,0:T(8,128)(2,1)S(1)}, u32[]{:S(2)}, u32[]{:S(2)}) collective-permute-start(bf16[2,256,768]{2,1,0:T(8,128)(2,1)S(1)} %fusion.79), channel_id=1, source_target_pairs={{0,2},{1,3},{2,0},{3,1},{4,6},{5,7},{6,4},{7,5},{8,10},{9,11},{10,... | collective-permute-start | bytes 2359304 | tf_op jit(solution)/shard_map/ppermute | solution.py:61
  68.6 18.0 %copy-start.34 = (f32[768]{0:T(1024)S(1)}, f32[768]{0:T(1024)}, u32[]{:S(2)}) copy-start(f32[768]{0:T(1024)} %param.24) | copy-start | bytes 9220
  68.6 18.0 %copy-start.41 = (f32[768]{0:T(1024)S(1)}, f32[768]{0:T(1024)}, u32[]{:S(2)}) copy-start(f32[768]{0:T(1024)} %param.25) | copy-start | bytes 9220
  68.6 34.1 %collective-permute-start.11 = (bf16[2,256,768]{2,1,0:T(8,128)(2,1)S(1)}, bf16[2,256,768]{2,1,0:T(8,128)(2,1)S(1)}, u32[]{:S(2)}, u32[]{:S(2)}) collective-permute-start(bf16[2,256,768]{2,1,0:T(8,128)(2,1)S(1)} %fusion.45), channel_id=1, source_target_pairs={{0,2},{1,3},{2,0},{3,1},{4,6},{5,7},{6,4},{7,5},{8,10},{9,11},{10,... | collective-permute-start | bytes 2359304 | tf_op jit(solution)/shard_map/ppermute | solution.py:34
  86.9 29.3 %collective-permute-start.4 = (bf16[2,256,768]{2,1,0:T(8,128)(2,1)S(1)}, bf16[2,256,768]{2,1,0:T(8,128)(2,1)S(1)}, u32[]{:S(2)}, u32[]{:S(2)}) collective-permute-start(bf16[2,256,768]{2,1,0:T(8,128)(2,1)S(1)} %add_convert_fusion.1), channel_id=1, source_target_pairs={{0,2},{1,3},{2,0},{3,1},{4,6},{5,7},{6,4},{7,5},{8,10},{9,11},{10,... | collective-permute-start | bytes 2359304 | tf_op jit(solution)/shard_map/ppermute | solution.py:34
  104.1 17.4 %collective-permute-start.12 = (bf16[2,2,256,768]{3,2,1,0:T(8,128)(2,1)}, bf16[2,2,256,768]{3,2,1,0:T(8,128)(2,1)}, u32[]{:S(2)}, u32[]{:S(2)}) collective-permute-start(bf16[2,2,256,768]{3,2,1,0:T(8,128)(2,1)} %maximum_select_fusion.8), channel_id=1, source_target_pairs={{0,1},{1,0},{2,3},{3,2},{4,5},{5,4},{6,7},{7,6},{8,9},{9,8},{10,11... | collective-permute-start | bytes 4718600 | tf_op jit(solution)/shard_map/ppermute | solution.py:38
  117.6 3.9 collective-permute-start.5
  131.0 2.8 copy-start.46
  138.3 6.4 %copy-start.48 = (bf16[2,768,768]{2,1,0:T(8,128)(2,1)S(1)}, bf16[2,768,768]{2,1,0:T(8,128)(2,1)}, u32[]{:S(2)}) copy-start(bf16[2,768,768]{2,1,0:T(8,128)(2,1)} %param.21) | copy-start | bytes 7077892
  149.2 15.0 %copy-start.18 = (bf16[2,2,2,256,768]{4,3,2,1,0:T(8,128)(2,1)S(1)}, bf16[2,2,2,256,768]{4,3,2,1,0:T(8,128)(2,1)}, u32[]{:S(2)}) copy-start(bf16[2,2,2,256,768]{4,3,2,1,0:T(8,128)(2,1)} %copy.56) | copy-start | bytes 9437188
  173.1 5.1 copy-start.47
  173.1 5.1 copy-start.51
  178.2 3.6 copy-start.49
  181.2 29.9 %collective-permute-start.13 = (bf16[2,2,256,768]{3,2,1,0:T(8,128)(2,1)S(1)}, bf16[2,2,256,768]{3,2,1,0:T(8,128)(2,1)S(1)}, u32[]{:S(2)}, u32[]{:S(2)}) collective-permute-start(bf16[2,2,256,768]{3,2,1,0:T(8,128)(2,1)S(1)} %fusion.38), channel_id=1, source_target_pairs={{0,1},{1,0},{2,3},{3,2},{4,5},{5,4},{6,7},{7,6},{8,9},{9,8},{10,11... | collective-permute-start | bytes 4718600 | tf_op jit(solution)/shard_map/ppermute | solution.py:57
  192.3 4.7 copy-start.13
  193.8 23.4 %collective-permute-start.6 = (bf16[2,2,256,768]{3,2,1,0:T(8,128)(2,1)}, bf16[2,2,256,768]{3,2,1,0:T(8,128)(2,1)}, u32[]{:S(2)}, u32[]{:S(2)}) collective-permute-start(bf16[2,2,256,768]{3,2,1,0:T(8,128)(2,1)} %fusion.39), channel_id=1, source_target_pairs={{0,1},{1,0},{2,3},{3,2},{4,5},{5,4},{6,7},{7,6},{8,9},{9,8},{10,11... | collective-permute-start | bytes 4718600 | tf_op jit(solution)/shard_map/ppermute | solution.py:57
  197.0 5.7 %copy-start.52 = (bf16[8,256,768]{2,1,0:T(8,128)(2,1)S(1)}, bf16[8,256,768]{2,1,0:T(8,128)(2,1)}, u32[]{:S(2)}) copy-start(bf16[8,256,768]{2,1,0:T(8,128)(2,1)} %add_convert_fusion) | copy-start | bytes 9437188
  202.7 2.8 copy-start.20
  211.4 4.2 copy-start.11
  212.5 20.7 %collective-permute-start.14 = (bf16[2,256,768]{2,1,0:T(8,128)(2,1)}, bf16[2,256,768]{2,1,0:T(8,128)(2,1)}, u32[]{:S(2)}, u32[]{:S(2)}) collective-permute-start(bf16[2,256,768]{2,1,0:T(8,128)(2,1)} %fusion.81), channel_id=1, source_target_pairs={{0,2},{1,3},{2,0},{3,1},{4,6},{5,7},{6,4},{7,5},{8,10},{9,11},{10,... | collective-permute-start | bytes 2359304 | tf_op jit(solution)/shard_map/ppermute | solution.py:61
  217.2 16.0 %copy-start.12 = (f32[2,2,256,768]{3,2,1,0:T(8,128)S(1)}, f32[2,2,256,768]{3,2,1,0:T(8,128)}, u32[]{:S(2)}) copy-start(f32[2,2,256,768]{3,2,1,0:T(8,128)} %copy-done.11) | copy-start | bytes 9437188
  220.1 28.9 %collective-permute-start.7 = (bf16[2,256,768]{2,1,0:T(8,128)(2,1)S(1)}, bf16[2,256,768]{2,1,0:T(8,128)(2,1)S(1)}, u32[]{:S(2)}, u32[]{:S(2)}) collective-permute-start(bf16[2,256,768]{2,1,0:T(8,128)(2,1)S(1)} %fusion.80), channel_id=1, source_target_pairs={{0,2},{1,3},{2,0},{3,1},{4,6},{5,7},{6,4},{7,5},{8,10},{9,11},{10,... | collective-permute-start | bytes 2359304 | tf_op jit(solution)/shard_map/ppermute | solution.py:61
  234.8 14.2 %copy-start.10 = (bf16[2,256,768]{2,1,0:T(8,128)(2,1)S(1)}, bf16[2,256,768]{2,1,0:T(8,128)(2,1)}, u32[]{:S(2)}) copy-start(bf16[2,256,768]{2,1,0:T(8,128)(2,1)} %param.14) | copy-start | bytes 2359300
  250.8 18.7 %collective-permute-start.15 = (bf16[2,256,768]{2,1,0:T(8,128)(2,1)S(1)}, bf16[2,256,768]{2,1,0:T(8,128)(2,1)S(1)}, u32[]{:S(2)}, u32[]{:S(2)}) collective-permute-start(bf16[2,256,768]{2,1,0:T(8,128)(2,1)S(1)} %convert_element_type.209), channel_id=1, source_target_pairs={{0,2},{1,3},{2,0},{3,1},{4,6},{5,7},{6,4},{7,5},{8,10},{9,11},{10,... | collective-permute-start | bytes 2359304 | tf_op jit(solution)/shard_map/ppermute | solution.py:34
  270.9 3.8 collective-permute-start.16
  270.9 253.2 %all-reduce.5.cloned.1.call-start = ((), (), s32[]{:S(2)}) async-start(), calls=%async_computation | async-start | bytes 2359296 | tf_op jit(solution)/shard_map/psum | solution.py:277
  274.6 5.4 %slice-start = ((s8[6291456]{0:T(1024)(128)(4,1)}), s8[4194304]{0:T(1024)(128)(4,1)S(1)}, s32[]{:S(2)}) async-start(s8[6291456]{0:T(1024)(128)(4,1)} %bitcast.268), calls=%async_computation.2 | async-start | bytes 8388608
  277.8 2.3 slice-start.1
  299.3 5.5 %copy-start.17 = (bf16[2,2,2,256,768]{4,3,2,1,0:T(8,128)(2,1)S(1)}, bf16[2,2,2,256,768]{4,3,2,1,0:T(8,128)(2,1)}, u32[]{:S(2)}) copy-start(bf16[2,2,2,256,768]{4,3,2,1,0:T(8,128)(2,1)} %copy-done.16) | copy-start | bytes 9437188
  299.3 3.5 collective-permute-start.17
  303.2 19.7 %collective-permute-start.18 = (bf16[2,256,768]{2,1,0:T(8,128)(2,1)S(1)}, bf16[2,256,768]{2,1,0:T(8,128)(2,1)S(1)}, u32[]{:S(2)}, u32[]{:S(2)}) collective-permute-start(bf16[2,256,768]{2,1,0:T(8,128)(2,1)S(1)} %fusion.82), channel_id=1, source_target_pairs={{0,2},{1,3},{2,0},{3,1},{4,6},{5,7},{6,4},{7,5},{8,10},{9,11},{10,... | collective-permute-start | bytes 2359304 | tf_op jit(solution)/shard_map/ppermute | solution.py:61
  304.8 18.1 %copy-start.33 = (f32[768]{0:T(1024)S(1)}, f32[768]{0:T(1024)}, u32[]{:S(2)}) copy-start(f32[768]{0:T(1024)} %param.22) | copy-start | bytes 9220
  304.8 18.1 %copy-start.36 = (f32[2,256]{1,0:T(2,128)S(1)}, f32[2,256]{1,0:T(2,128)}, u32[]{:S(2)}) copy-start(f32[2,256]{1,0:T(2,128)} %copy-done.35) | copy-start | bytes 6148
  307.8 15.9 %copy-start.44 = (f32[2,256]{1,0:T(2,128)S(1)}, f32[2,256]{1,0:T(2,128)}, u32[]{:S(2)}) copy-start(f32[2,256]{1,0:T(2,128)} %copy-done.43) | copy-start | bytes 6148
  307.8 17.0 %copy-start.38 = (f32[2,256]{1,0:T(2,128)S(1)}, f32[2,256]{1,0:T(2,128)}, u32[]{:S(2)}) copy-start(f32[2,256]{1,0:T(2,128)} %copy-done.37) | copy-start | bytes 6148
  323.6 2.2 copy-start.15
  325.7 114.3 %collective-permute-start.19 = (f32[4,768]{1,0:T(4,128)S(1)}, f32[4,768]{1,0:T(4,128)S(1)}, u32[]{:S(2)}, u32[]{:S(2)}) collective-permute-start(f32[4,768]{1,0:T(4,128)S(1)} %pad_maximum_fusion.2), channel_id=1, source_target_pairs={{0,1},{1,0},{2,3},{3,2},{4,5},{5,4},{6,7},{7,6},{8,9},{9,8},{10,11... | collective-permute-start | bytes 36872 | tf_op jit(solution)/shard_map/ppermute | solution.py:72
  440.1 3.8 collective-permute-start.20
  443.8 5.8 %copy-start.28 = (bf16[2,768,768]{2,1,0:T(8,128)(2,1)S(1)}, bf16[2,768,768]{2,1,0:T(8,128)(2,1)}, u32[]{:S(2)}) copy-start(bf16[2,768,768]{2,1,0:T(8,128)(2,1)} %get-tuple-element.24) | copy-start | bytes 7077892
  443.9 8.3 %collective-permute-start.21 = (f32[4,768]{1,0:T(4,128)S(1)}, f32[4,768]{1,0:T(4,128)S(1)}, u32[]{:S(2)}, u32[]{:S(2)}) collective-permute-start(f32[4,768]{1,0:T(4,128)S(1)} %fusion.126), channel_id=1, source_target_pairs={{0,4},{4,0},{8,12},{12,8},{16,20},{20,16},{24,28},{28,24},{1,5},{5... | collective-permute-start | bytes 36872 | tf_op jit(solution)/shard_map/ppermute | solution.py:72
  449.6 8.2 %copy-start.7 = (f32[2,256,768]{2,1,0:T(8,128)S(1)}, f32[2,256,768]{2,1,0:T(8,128)}, u32[]{:S(2)}) copy-start(f32[2,256,768]{2,1,0:T(8,128)} %copy-done.6) | copy-start | bytes 4718596
  452.2 3.9 collective-permute-start.22
  456.0 4.9 collective-permute-start.23
  524.1 2.6 copy-start.31
  (17 other events, 23.1 us)
Sparse Core Ops, SparseCore 0:
  271.1 168.8 all-reduce.6
  444.1 79.9 all-reduce.4

commit v3 on v2

--- a/solution.py
+++ b/solution.py
@@ -2,6 +2,7 @@
 import jax.numpy as jnp
 from jax import lax
 from jax.sharding import PartitionSpec as P
+
 
 HD = 64
 
@@ -42,11 +43,12 @@
     return quad.reshape((-1,) + values.shape[1:])
 
 
-def scatter_rows_mp(partial):
+def scatter_rows_mp(partial, tie=None):
     if lax.axis_size("mp") != 4:
-        return lax.psum_scatter(
+        result = lax.psum_scatter(
             partial.astype(jnp.bfloat16), "mp", scatter_dimension=0, tiled=True
         ).astype(jnp.float32)
+        return result if tie is None else (result, tie)
     index = lax.axis_index("mp")
     chip_y = index // 2
     core = index % 2
@@ -59,7 +61,10 @@
     keep_y = lax.dynamic_index_in_dim(chip_sum, chip_y, axis=0, keepdims=False)
     send_y = lax.dynamic_index_in_dim(chip_sum, 1 - chip_y, axis=0, keepdims=False)
     got_y = lax.ppermute(send_y.astype(jnp.bfloat16), "mp", xor_pairs(4, 2))
-    return keep_y + got_y.astype(jnp.float32)
+    if tie is not None:
+        tie, got_y = lax.optimization_barrier((tie, got_y))
+    result = keep_y + got_y.astype(jnp.float32)
+    return result if tie is None else (result, tie)
 
 
 def butterfly_sum(values, axis):
@@ -73,6 +78,41 @@
         )
         bit *= 2
     return values
+
+
+def butterfly_allreduce_low(values, axis):
+    size = lax.axis_size(axis)
+    flat = jnp.concatenate([v.reshape(-1).astype(jnp.float32) for v in values])
+    if size & (size - 1) or flat.shape[0] % size:
+        summed = lax.psum(flat.astype(jnp.bfloat16), axis)
+    else:
+        steps = size.bit_length() - 1
+        index = lax.axis_index(axis)
+        chunk = flat.shape[0] // size
+        held = flat.reshape((2,) * steps + (chunk,))
+        for step in range(steps):
+            bit = 1 << step
+            mine = (index // bit) % 2
+            last = steps - 1 - step
+            keep = lax.dynamic_index_in_dim(held, mine, axis=last, keepdims=False)
+            send = lax.dynamic_index_in_dim(held, 1 - mine, axis=last, keepdims=False)
+            got = lax.ppermute(send.astype(jnp.bfloat16), axis, xor_pairs(size, bit))
+            held = keep + got.astype(jnp.float32)
+        held = held.astype(jnp.bfloat16)
+        for step in reversed(range(steps)):
+            bit = 1 << step
+            mine = (index // bit) % 2
+            got = lax.ppermute(held, axis, xor_pairs(size, bit))
+            place = steps - 1 - step
+            held = jnp.where(
+                mine == 0, jnp.stack([held, got], axis=place), jnp.stack([got, held], axis=place)
+            )
+        summed = held.reshape(-1)
+    out, start = [], 0
+    for v in values:
+        out.append(summed[start : start + v.size].reshape(v.shape).astype(jnp.float32))
+        start += v.size
+    return tuple(out)
 
 
 def select_rows(values, hot_column):
@@ -166,8 +206,7 @@
             down_weight[ffn_expert],
             preferred_element_type=jnp.float32,
         )
-    ffn_local = scatter_rows_mp(total)
-    output = (residual + ffn_local).astype(jnp.bfloat16)
+    ffn_partial = total
     count_float = counts.astype(jnp.float32)
     loss_weight = jnp.sum(count_float) / (experts * count_float)
     local_hot = lax.dynamic_slice_in_dim(expert_hot, first_row, local_rows, 0)
@@ -203,6 +242,8 @@
         )
     grad_in_weight = jnp.stack(in_list, axis=0)
     ffn_grads = (grad_in_weight.astype(jnp.bfloat16), grad_down_weight.astype(jnp.bfloat16))
+    ffn_grads, grad_up = lax.optimization_barrier((ffn_grads, grad_up))
+    ffn_summed = lax.psum(ffn_grads, "dp")
     picked = grad_up
     hot_picked = hot_matrix
     total = jnp.zeros((local_rows * lax.axis_size("mp"), slots, model_width), jnp.float32)
@@ -217,9 +258,9 @@
     second_back = jax.vjp(layer_norm, residual, gain_ffn, shift_ffn)[1]
     grad_from_second, grad_gain_ffn, grad_shift_ffn = second_back(grad_norm_two)
     grad_residual = grad_output + grad_from_second
-    ffn_grads, grad_residual = lax.optimization_barrier((ffn_grads, grad_residual))
-    ffn_summed = lax.psum(ffn_grads, "dp")
     grad_attn_full = gather_rows_mp(grad_residual.astype(jnp.bfloat16))
+    ffn_partial, grad_attn_full = lax.optimization_barrier((ffn_partial, grad_attn_full))
+    output = (residual + scatter_rows_mp(ffn_partial)).astype(jnp.bfloat16)
     grad_out_weight = jnp.einsum(
         "rsk,rsd->kd", head_mix, grad_attn_full, preferred_element_type=jnp.float32
     )
@@ -271,11 +312,8 @@
         ),
         "dp",
     )
-    attn_grads, ffn_summed = lax.optimization_barrier(
-        ((grad_qkv_weight.astype(jnp.bfloat16), grad_out_weight.astype(jnp.bfloat16)), ffn_summed)
-    )
-    attn_summed = lax.psum(attn_grads, "dp")
-    summed = tuple(g.astype(jnp.float32) for g in attn_summed + ffn_summed)
+    attn_summed = butterfly_allreduce_low((grad_qkv_weight, grad_out_weight), "dp")
+    summed = attn_summed + tuple(g.astype(jnp.float32) for g in ffn_summed)
     return (
         output,
         grad_tokens,
@@ -320,6 +358,5 @@
         P(),
         P(),
     )
-    return jax.shard_map(
-        per_device, mesh=mesh, in_specs=in_specs, out_specs=out_specs, check_vma=False
-    )
+
+    return jax.shard_map(per_device, mesh=mesh, in_specs=in_specs, out_specs=out_specs, check_vma=False)

time: 538 us -> 524 us (0.974)
  waiting for transfers between devices: 310 us -> 232 us
  local copies, waits for them, and re-layouts: 20.8 us -> 60.2 us
  other arithmetic: 82.4 us -> 101 us
    psum x1 -> x0, waiting for transfers between devices: 62.5 us -> none  [per_device(): attn_summed = lax.psum(attn_grads, 'dp')]
    ppermute x0 -> x6, waiting for transfers between devices: none -> 33.7 us  [the longest x3 18.9 us: butterfly_allreduce_low(): got = lax.ppermute(held, axis, xor_pairs(size, bit))]
    psum x1, waiting for transfers between devices: 113 us -> 89.3 us  [per_device(): ffn_summed = lax.psum(ffn_grads, 'dp')]
    ppermute x4, waiting for transfers between devices: 57.4 us -> 36.8 us  [scatter_rows_mp(): got_y = lax.ppermute(send_y.astype(jnp.bfloat16), 'mp', xor_pairs(4, 2))]
    select_n x0 -> x3, local copies, waits for them, and re-layouts: none -> 10.5 us  [butterfly_allreduce_low(): jnp.where(mine == 0, jnp.stack([held, got], axis=place), jnp.stack([got,...]
    unnamed x110 -> x141, local copies, waits for them, and re-layouts: 13.2 us -> 22 us
    select_n x0 -> x5, other arithmetic: none -> 6.1 us  [butterfly_allreduce_low(): jnp.where(mine == 0, jnp.stack([held, got], axis=place), jnp.stack([got,...]
    reshape x0 -> x2, local copies, waits for them, and re-layouts: none -> 5.8 us  [the longest x1 4.7 us: butterfly_allreduce_low(): held = flat.reshape((2,) * steps + (chunk,))]
  transfers between devices with their start and end apart: 26 -> 31, of which waited for: 18 -> 20; matrix products, arithmetic and copies ran while one was open for 17% -> 24% of each run, Pallas kernels for 0% -> 0%
where the time goes in v3:
time: 524 us; the launch traced here: 520 us
  waiting for transfers between devices  232 us (44%)
  other arithmetic  101 us (19%)
  matrix products  81.7 us (16%)
  local copies, waits for them, and re-layouts  60.2 us (11%)
  starting transfers between devices  29.5 us (6%)
  between operations  15.6 us (3%)
    psum x1, waiting for transfers between devices, per_device(): ffn_summed = lax.psum(ffn_grads, 'dp')  89.3 us
    ppermute x4, waiting for transfers between devices, gather_rows_mp(): other_y = lax.ppermute(values, 'mp', xor_pairs(4, 2))  60.6 us
    ppermute x4, waiting for transfers between devices, scatter_rows_mp(): got_y = lax.ppermute(send_y.astype(jnp.bfloat16), 'mp', xor_pairs(4, 2))  36.8 us
    unnamed x141, local copies, waits for them, and re-layouts  22 us
    ppermute x3, waiting for transfers between devices, butterfly_allreduce_low(): got = lax.ppermute(held, axis, xor_pairs(size, bit))  18.9 us
    dot_general x2, matrix products, per_device(): jnp.einsum('rsd,fd->rsf', masked_grad, down_weight[expert], preferred_ele...  15.6 us
    convert_element_type x1, other arithmetic, per_device(): activated = gelu_exact(upward).astype(jnp.bfloat16)  14.9 us
    ppermute x3, waiting for transfers between devices, butterfly_allreduce_low(): got = lax.ppermute(send.astype(jnp.bfloat16), axis, xor_pairs(size, bit))  14.9 us
  transfers between devices with their start and end apart: 31, of which 20 were waited for; matrix products, arithmetic and copies ran while one was open for 24% of the time, Pallas kernels for 0%

profile of v3, /device:TPU:0, one launch (start us, length us, event | category | flops | bytes accessed | tf_op | source)
XLA Modules:
  0.0 520.0 jit_solution(18194335441972745900)
XLA Ops:
  10.3 2.4 fusion.33
  12.6 3.0 collective-permute-start
  16.0 17.4 %collective-permute-done = bf16[2,256,768]{2,1,0:T(8,128)(2,1)S(1)} collective-permute-done((bf16[2,256,768]{2,1,0:T(8,128)(2,1)}, bf16[2,256,768]{2,1,0:T(8,128)(2,1)S(1)}, u32[]{:S(2)}, u32[]{:S(2)}) %collective-permute-start) | collective-permute-done | bytes 786464 | tf_op jit(solution)/shard_map/ppermute | solution.py:35
  38.5 2.6 maximum_select_fusion
  41.4 2.0 convolution_convert_fusion
  49.7 2.6 copy-done.6
  55.8 1.8 collective-permute-done.6
  61.3 2.8 collective-permute-start.8
  64.1 2.2 bitcast_add_fusion.3
  70.2 16.7 %collective-permute-done.3 = bf16[2,256,768]{2,1,0:T(8,128)(2,1)S(1)} collective-permute-done((bf16[2,256,768]{2,1,0:T(8,128)(2,1)S(1)}, bf16[2,256,768]{2,1,0:T(8,128)(2,1)S(1)}, u32[]{:S(2)}, u32[]{:S(2)}) %collective-permute-start.3) | collective-permute-done | bytes 786464 | tf_op jit(solution)/shard_map/ppermute | solution.py:63
  89.7 14.0 %collective-permute-done.9 = bf16[2,256,768]{2,1,0:T(8,128)(2,1)S(1)} collective-permute-done((bf16[2,256,768]{2,1,0:T(8,128)(2,1)S(1)}, bf16[2,256,768]{2,1,0:T(8,128)(2,1)S(1)}, u32[]{:S(2)}, u32[]{:S(2)}) %collective-permute-start.9) | collective-permute-done | bytes 786464 | tf_op jit(solution)/shard_map/ppermute | solution.py:35
  105.4 12.0 %collective-permute-done.4 = bf16[2,256,768]{2,1,0:T(8,128)(2,1)S(1)} collective-permute-done((bf16[2,256,768]{2,1,0:T(8,128)(2,1)S(1)}, bf16[2,256,768]{2,1,0:T(8,128)(2,1)S(1)}, u32[]{:S(2)}, u32[]{:S(2)}) %collective-permute-start.4) | collective-permute-done | bytes 786464 | tf_op jit(solution)/shard_map/ppermute | solution.py:35
  122.5 6.1 %broadcast_multiply_fusion = (bf16[2,2,2,256,768]{4,3,2,0,1:T(8,128)(2,1)S(1)}, bf16[2,2,2,256,768]{4,3,2,0,1:T(8,128)(2,1)S(1)}, bf16[2,2,2,256,768]{4,3,2,0,1:T(8,128)(2,1)}, bf16[2,2,2,256,768]{4,3,2,0,1:T(8,128)(2,1)S(1)}) fusion(bf16[2,2,2]{2,0,1:T(2,128)(2,1)S(1)} %copy.89, bf16[2,1,2,256,768]{4,3,2,0,1:T(8,128)(2,1)S(1)} %maximum_select_fusion.7, ...), kind=kLoop, calls=%fused_computation.125 | loop fusion | flops 12582912 | bytes 18874384 | tf_op jit(solution)/shard_map/mul | solution.py:119
  133.1 4.5 fusion.73
  137.6 6.2 %fusion.51 = (u8[256,768]{1,0:T(8,128)(4,1)S(1)}, u8[256,768]{1,0:T(8,128)(4,1)S(1)}, f32[8,256,768]{2,1,0:T(8,128)S(1)}) fusion(f32[8,256,768]{2,1,0:T(8,128)} %fusion.73, bf16[8,256,768]{2,1,0:T(8,128)(2,1)S(1)} %bitcast.299, bf16[2,768,768]{2,1,0:T(8,128)(2,1)S(1)} %copy-done.52), kind=kOutput, calls=%fused_computation.133 | convolution fusion | flops 2437545984 | bytes 17301504 | tf_op jit(solution)/shard_map/rsd,df->rsf/dot_general | solution.py:192
  143.9 14.9 %multiply_convert_fusion.1 = (bf16[8,256,768]{2,1,0:T(8,128)(2,1)S(1)}, f32[8,256,768]{2,1,0:T(8,128)}) fusion(f32[8,256,768]{2,1,0:T(8,128)S(1)} %get-tuple-element.91, u8[256,768]{1,0:T(8,128)(4,1)S(1)} %get-tuple-element.44, u8[256,768]{1,0:T(8,128)(4,1)S(1)} %get-tuple-element.43), kind=kLoop, calls=%fused_computation.11 | loop fusion | flops 110100480 | bytes 16121856 | tf_op jit(solution)/shard_map/convert_element_type | solution.py:198
  158.8 3.7 bitcast_multiply_fusion.3
  162.4 3.7 fusion.54
  166.2 3.7 fusion.55
  170.1 1.9 copy.93
  172.1 5.0 fusion.67
  178.7 10.6 %add_convert_fusion = bf16[8,256,768]{2,1,0:T(8,128)(2,1)} fusion(f32[8,256,768]{2,1,0:T(8,128)S(1)} %bitcast.288, f32[8,256,768]{2,1,0:T(8,128)} %fusion.67, f32[8,256,768]{2,1,0:T(8,128)S(1)} %bitcast.286, bf16[8,256,768]{2,1,0:T(8,128)(2,1)} %bitcast.300, bf16[2,768,768]{2,1,0:T(8,128)(2,1)} %param.21), kind=kOutput, calls=%fused_computation.10 | convolution fusion | flops 2439512064 | bytes 26345472 | tf_op jit(solution)/shard_map/rsd,fd->rsf/dot_general | solution.py:225
  189.3 4.8 fusion.52
  194.1 2.8 fusion.53
  196.9 2.5 pad_maximum_fusion
  199.5 5.1 fusion.11
  204.6 2.7 fusion.27
  207.7 3.3 collective-permute-done.11
  213.0 18.1 %collective-permute-done.12 = bf16[2,256,768]{2,1,0:T(8,128)(2,1)S(1)} collective-permute-done((bf16[2,256,768]{2,1,0:T(8,128)(2,1)S(1)}, bf16[2,256,768]{2,1,0:T(8,128)(2,1)S(1)}, u32[]{:S(2)}, u32[]{:S(2)}) %collective-permute-start.12) | collective-permute-done | bytes 786464 | tf_op jit(solution)/shard_map/ppermute | solution.py:63
  235.5 17.4 %collective-permute-done.13 = bf16[2,256,768]{2,1,0:T(8,128)(2,1)S(1)} collective-permute-done((bf16[2,256,768]{2,1,0:T(8,128)(2,1)}, bf16[2,256,768]{2,1,0:T(8,128)(2,1)S(1)}, u32[]{:S(2)}, u32[]{:S(2)}) %collective-permute-start.13) | collective-permute-done | bytes 786464 | tf_op jit(solution)/shard_map/ppermute | solution.py:35
  254.7 4.1 fusion.15
  258.8 4.6 fusion.24
  270.2 4.2 multiply_reduce_fusion
  274.3 4.5 multiply_convert_fusion
  282.1 2.7 fusion.105
  284.8 2.7 copy-done.18
  289.9 3.9 convolution_bitcast_fusion
  293.8 3.1 reshape_reshape.3
  296.9 3.5 convolution_bitcast_fusion.1
  301.5 3.0 pad_maximum_fusion.3
  304.5 4.7 reshape.746
  309.3 2.9 dynamic-slice_convert_fusion.5
  314.7 2.2 constant_dynamic-slice_fusion.2
  317.0 89.3 %all-reduce.3.cloned.1.call-done = (bf16[2,768,768]{2,1,0:T(8,128)(2,1)}, bf16[2,768,768]{2,1,0:T(8,128)(2,1)}) async-done(((bf16[2,768,768]{2,1,0:T(8,128)(2,1)}, bf16[2,768,768]{2,1,0:T(8,128)(2,1)}), (bf16[2,768,768]{2,1,0:T(8,128)(2,1)}, bf16[2,768,768]{2,1,0:T(8,128)(2,1)})) %all-reduce.3.cloned.1.call-update) | async-done | bytes 4718608 | tf_op jit(solution)/shard_map/psum | solution.py:246
  406.2 4.4 convert_element_type.262
  410.6 2.8 convert_element_type.263
  413.4 2.7 bitcast_add_fusion.8
  417.8 7.9 %collective-permute-done.20 = bf16[2,73728]{1,0:T(2,128)(2,1)S(1)} collective-permute-done((bf16[2,73728]{1,0:T(2,128)(2,1)S(1)}, bf16[2,73728]{1,0:T(2,128)(2,1)S(1)}, u32[]{:S(2)}, u32[]{:S(2)}) %collective-permute-start.20) | collective-permute-done | bytes 294944 | tf_op jit(solution)/shard_map/ppermute | solution.py:99
  428.9 6.9 %collective-permute-done.21 = bf16[73728]{0:T(1024)(128)(2,1)S(1)} collective-permute-done((bf16[73728]{0:T(1024)(128)(2,1)S(1)}, bf16[73728]{0:T(1024)(128)(2,1)S(1)}, u32[]{:S(2)}, u32[]{:S(2)}) %collective-permute-start.21) | collective-permute-done | bytes 147488 | tf_op jit(solution)/shard_map/ppermute | solution.py:99
  436.5 7.8 %collective-permute-done.22 = bf16[73728]{0:T(1024)(128)(2,1)S(1)} collective-permute-done((bf16[73728]{0:T(1024)(128)(2,1)S(1)}, bf16[73728]{0:T(1024)(128)(2,1)S(1)}, u32[]{:S(2)}, u32[]{:S(2)}) %collective-permute-start.22) | collective-permute-done | bytes 147488 | tf_op jit(solution)/shard_map/ppermute | solution.py:105
  448.9 5.9 %collective-permute-done.23 = bf16[2,73728]{1,0:T(2,128)(2,1)S(1)} collective-permute-done((bf16[2,73728]{1,0:T(2,128)(2,1)S(1)}, bf16[2,73728]{1,0:T(2,128)(2,1)S(1)}, u32[]{:S(2)}, u32[]{:S(2)}) %collective-permute-start.23) | collective-permute-done | bytes 294944 | tf_op jit(solution)/shard_map/ppermute | solution.py:105
  455.7 1.9 collective-permute-start.24
  465.1 5.2 collective-permute-done.24
  473.3 2.2 copy.114
  475.5 4.5 select_n.370
  480.0 2.0 collective-permute-done.18
  482.1 2.1 fusion.36
  486.4 2.1 slice_convert_fusion
  488.5 3.8 select_n.371
  495.7 4.2 copy.116
  500.6 3.1 collective-permute-done.27
  504.1 3.6 add_add_fusion.2
  507.6 2.2 collective-permute-start.29
  509.8 2.4 fusion.44
  (297 shorter events, 95.0 us)
Async XLA Ops:
  7.2 34.2 %copy-start = (bf16[768,3,192]{0,2,1:T(8,128)(2,1)S(1)}, bf16[768,3,192]{0,2,1:T(8,128)(2,1)}, u32[]{:S(2)}) copy-start(bf16[768,3,192]{0,2,1:T(8,128)(2,1)} %param.18) | copy-start | bytes 2654212
  7.2 8.4 %copy-start.2 = (bf16[2,256,768]{2,1,0:T(8,128)(2,1)S(1)}, bf16[2,256,768]{2,1,0:T(8,128)(2,1)}, u32[]{:S(2)}) copy-start(bf16[2,256,768]{2,1,0:T(8,128)(2,1)} %param.13) | copy-start | bytes 2359300
  7.2 8.4 %copy-start.38 = (f32[768]{0:T(1024)S(1)}, f32[768]{0:T(1024)}, u32[]{:S(2)}) copy-start(f32[768]{0:T(1024)} %param.22) | copy-start | bytes 9220
  7.2 8.4 %copy-start.46 = (f32[768]{0:T(1024)S(1)}, f32[768]{0:T(1024)}, u32[]{:S(2)}) copy-start(f32[768]{0:T(1024)} %param.23) | copy-start | bytes 9220
  7.2 399.0 %all-reduce.3.cloned.1.call-start = ((), (), s32[]{:S(2)}) async-start(), calls=%async_computation | async-start | bytes 9437184 | tf_op jit(solution)/shard_map/psum | solution.py:246
  8.7 26.9 %copy-start.40 = (f32[2,256]{1,0:T(2,128)}, f32[2,256]{1,0:T(2,128)S(1)}, u32[]{:S(2)}) copy-start(f32[2,256]{1,0:T(2,128)S(1)} %broadcast_multiply_fusion.5) | copy-start | bytes 6148
  10.2 5.4 %copy-start.49 = (f32[2,256]{1,0:T(2,128)}, f32[2,256]{1,0:T(2,128)S(1)}, u32[]{:S(2)}) copy-start(f32[2,256]{1,0:T(2,128)S(1)} %fusion.35) | copy-start | bytes 6148
  10.2 25.3 %copy-start.43 = (f32[2,256]{1,0:T(2,128)}, f32[2,256]{1,0:T(2,128)S(1)}, u32[]{:S(2)}) copy-start(f32[2,256]{1,0:T(2,128)S(1)} %fusion.95) | copy-start | bytes 6148
  12.6 20.7 %collective-permute-start = (bf16[2,256,768]{2,1,0:T(8,128)(2,1)}, bf16[2,256,768]{2,1,0:T(8,128)(2,1)S(1)}, u32[]{:S(2)}, u32[]{:S(2)}) collective-permute-start(bf16[2,256,768]{2,1,0:T(8,128)(2,1)} %fusion.33), channel_id=1, source_target_pairs={{0,2},{1,3},{2,0},{3,1},{4,6},{5,7},{6,4},{7,5},{8,10},{9,11},{10,... | collective-permute-start | bytes 2359304 | tf_op jit(solution)/shard_map/ppermute | solution.py:35
  15.6 19.2 %copy-start.45 = (s32[8,256]{1,0:T(8,128)S(1)}, s32[8,256]{1,0:T(8,128)}, u32[]{:S(2)}) copy-start(s32[8,256]{1,0:T(8,128)} %param.16) | copy-start | bytes 24580
  15.7 19.2 %copy-start.48 = (s32[8,256]{1,0:T(8,128)S(1)}, s32[8,256]{1,0:T(8,128)}, u32[]{:S(2)}) copy-start(s32[8,256]{1,0:T(8,128)} %param.15) | copy-start | bytes 24580
  34.8 3.8 collective-permute-start.1
  53.7 10.4 %collective-permute-start.2 = (bf16[2,2,256,768]{3,2,1,0:T(8,128)(2,1)}, bf16[2,2,256,768]{3,2,1,0:T(8,128)(2,1)S(1)}, u32[]{:S(2)}, u32[]{:S(2)}) collective-permute-start(bf16[2,2,256,768]{3,2,1,0:T(8,128)(2,1)} %fusion.37), channel_id=1, source_target_pairs={{0,1},{1,0},{2,3},{3,2},{4,5},{5,4},{6,7},{7,6},{8,9},{9,8},{10,11... | collective-permute-start | bytes 4718600 | tf_op jit(solution)/shard_map/ppermute | solution.py:59
  54.1 3.6 collective-permute-start.6
  57.7 3.6 collective-permute-start.7
  61.3 8.0 %copy-start.4 = (bf16[2,256,768]{2,1,0:T(8,128)(2,1)S(1)}, bf16[2,256,768]{2,1,0:T(8,128)(2,1)}, u32[]{:S(2)}) copy-start(bf16[2,256,768]{2,1,0:T(8,128)(2,1)} %param.14) | copy-start | bytes 2359300
  61.3 6.7 %collective-permute-start.8 = (s32[2]{0:T(128)S(1)}, s32[2]{0:T(128)S(1)}, u32[]{:S(2)}, u32[]{:S(2)}) collective-permute-start(s32[2]{0:T(128)S(1)} %add.232), channel_id=1, source_target_pairs={{0,16},{4,20},{8,24},{12,28},{16,0},{20,4},{24,8},{28,12},{1,17},{... | collective-permute-start | bytes 32 | tf_op jit(solution)/shard_map/ppermute | solution.py:77
  66.4 20.5 %collective-permute-start.3 = (bf16[2,256,768]{2,1,0:T(8,128)(2,1)S(1)}, bf16[2,256,768]{2,1,0:T(8,128)(2,1)S(1)}, u32[]{:S(2)}, u32[]{:S(2)}) collective-permute-start(bf16[2,256,768]{2,1,0:T(8,128)(2,1)S(1)} %fusion.84), channel_id=1, source_target_pairs={{0,2},{1,3},{2,0},{3,1},{4,6},{5,7},{6,4},{7,5},{8,10},{9,11},{10,... | collective-permute-start | bytes 2359304 | tf_op jit(solution)/shard_map/ppermute | solution.py:63
  68.6 18.7 %copy-start.51 = (s32[2]{0:T(128)}, s32[2]{0:T(128)S(1)}, u32[]{:S(2)}) copy-start(s32[2]{0:T(128)S(1)} %get-tuple-element.66) | copy-start | bytes 28
  69.6 18.0 %copy-start.42 = (f32[768]{0:T(1024)S(1)}, f32[768]{0:T(1024)}, u32[]{:S(2)}) copy-start(f32[768]{0:T(1024)} %param.24) | copy-start | bytes 9220
  69.6 18.0 %copy-start.47 = (f32[768]{0:T(1024)S(1)}, f32[768]{0:T(1024)}, u32[]{:S(2)}) copy-start(f32[768]{0:T(1024)} %param.25) | copy-start | bytes 9220
  69.6 34.1 %collective-permute-start.9 = (bf16[2,256,768]{2,1,0:T(8,128)(2,1)S(1)}, bf16[2,256,768]{2,1,0:T(8,128)(2,1)S(1)}, u32[]{:S(2)}, u32[]{:S(2)}) collective-permute-start(bf16[2,256,768]{2,1,0:T(8,128)(2,1)S(1)} %fusion.45), channel_id=1, source_target_pairs={{0,2},{1,3},{2,0},{3,1},{4,6},{5,7},{6,4},{7,5},{8,10},{9,11},{10,... | collective-permute-start | bytes 2359304 | tf_op jit(solution)/shard_map/ppermute | solution.py:35
  87.9 29.5 %collective-permute-start.4 = (bf16[2,256,768]{2,1,0:T(8,128)(2,1)S(1)}, bf16[2,256,768]{2,1,0:T(8,128)(2,1)S(1)}, u32[]{:S(2)}, u32[]{:S(2)}) collective-permute-start(bf16[2,256,768]{2,1,0:T(8,128)(2,1)S(1)} %add_convert_fusion.1), channel_id=1, source_target_pairs={{0,2},{1,3},{2,0},{3,1},{4,6},{5,7},{6,4},{7,5},{8,10},{9,11},{10,... | collective-permute-start | bytes 2359304 | tf_op jit(solution)/shard_map/ppermute | solution.py:35
  105.1 13.9 %copy-start.5 = (bf16[2,256,768]{2,1,0:T(8,128)(2,1)S(1)}, bf16[2,256,768]{2,1,0:T(8,128)(2,1)}, u32[]{:S(2)}) copy-start(bf16[2,256,768]{2,1,0:T(8,128)(2,1)} %param.14) | copy-start | bytes 2359300
  105.1 16.5 %collective-permute-start.10 = (bf16[2,2,256,768]{3,2,1,0:T(8,128)(2,1)}, bf16[2,2,256,768]{3,2,1,0:T(8,128)(2,1)}, u32[]{:S(2)}, u32[]{:S(2)}) collective-permute-start(bf16[2,2,256,768]{3,2,1,0:T(8,128)(2,1)} %maximum_select_fusion.8), channel_id=1, source_target_pairs={{0,1},{1,0},{2,3},{3,2},{4,5},{5,4},{6,7},{7,6},{8,9},{9,8},{10,11... | collective-permute-start | bytes 4718600 | tf_op jit(solution)/shard_map/ppermute | solution.py:39
  118.8 3.8 collective-permute-start.5
  143.9 14.9 %copy-start.16 = (f32[8,256,768]{2,1,0:T(8,128)}, f32[8,256,768]{2,1,0:T(8,128)S(1)}, u32[]{:S(2)}) copy-start(f32[8,256,768]{2,1,0:T(8,128)S(1)} %get-tuple-element.91) | copy-start | bytes 18874372
  158.8 7.4 %copy-start.25 = (bf16[8,256,768]{2,1,0:T(8,128)(2,1)}, bf16[8,256,768]{2,1,0:T(8,128)(2,1)S(1)}, u32[]{:S(2)}) copy-start(bf16[8,256,768]{2,1,0:T(8,128)(2,1)S(1)} %get-tuple-element.67) | copy-start | bytes 9437188
  170.1 7.0 %slice-start.2 = ((s8[6291456]{0:T(1024)(128)(4,1)}), s8[4194304]{0:T(1024)(128)(4,1)S(1)}, s32[]{:S(2)}) async-start(s8[6291456]{0:T(1024)(128)(4,1)} %bitcast.285), calls=%async_computation.3 | async-start | bytes 8388608
  170.1 7.0 %slice-start.4 = ((s8[6291456]{0:T(1024)(128)(4,1)}), s8[4194304]{0:T(1024)(128)(4,1)S(1)}, s32[]{:S(2)}) async-start(s8[6291456]{0:T(1024)(128)(4,1)} %bitcast.287), calls=%async_computation.5 | async-start | bytes 8388608
  172.1 6.0 %slice-start.3 = ((s8[6291456]{0:T(1024)(128)(4,1)}), s8[2097152]{0:T(1024)(128)(4,1)S(1)}, s32[]{:S(2)}) async-start(s8[6291456]{0:T(1024)(128)(4,1)} %bitcast.285), calls=%async_computation.4 | async-start | bytes 4194304
  172.1 6.5 %slice-start.5 = ((s8[6291456]{0:T(1024)(128)(4,1)}), s8[2097152]{0:T(1024)(128)(4,1)S(1)}, s32[]{:S(2)}) async-start(s8[6291456]{0:T(1024)(128)(4,1)} %bitcast.287), calls=%async_computation.6 | async-start | bytes 4194304
  178.7 10.6 %copy-start.20 = (bf16[8,256,768]{2,1,0:T(8,128)(2,1)S(1)}, bf16[8,256,768]{2,1,0:T(8,128)(2,1)}, u32[]{:S(2)}) copy-start(bf16[8,256,768]{2,1,0:T(8,128)(2,1)} %get-tuple-element.75) | copy-start | bytes 9437188
  207.5 3.5 collective-permute-start.11
  211.4 19.7 %collective-permute-start.12 = (bf16[2,256,768]{2,1,0:T(8,128)(2,1)S(1)}, bf16[2,256,768]{2,1,0:T(8,128)(2,1)S(1)}, u32[]{:S(2)}, u32[]{:S(2)}) collective-permute-start(bf16[2,256,768]{2,1,0:T(8,128)(2,1)S(1)} %fusion.85), channel_id=1, source_target_pairs={{0,2},{1,3},{2,0},{3,1},{4,6},{5,7},{6,4},{7,5},{8,10},{9,11},{10,... | collective-permute-start | bytes 2359304 | tf_op jit(solution)/shard_map/ppermute | solution.py:63
  233.9 18.9 %collective-permute-start.13 = (bf16[2,256,768]{2,1,0:T(8,128)(2,1)}, bf16[2,256,768]{2,1,0:T(8,128)(2,1)S(1)}, u32[]{:S(2)}, u32[]{:S(2)}) collective-permute-start(bf16[2,256,768]{2,1,0:T(8,128)(2,1)} %fusion.83), channel_id=1, source_target_pairs={{0,2},{1,3},{2,0},{3,1},{4,6},{5,7},{6,4},{7,5},{8,10},{9,11},{10,... | collective-permute-start | bytes 2359304 | tf_op jit(solution)/shard_map/ppermute | solution.py:35
  235.5 19.1 %copy-start.26 = (bf16[8,256,768]{2,1,0:T(8,128)(2,1)S(1)}, bf16[8,256,768]{2,1,0:T(8,128)(2,1)}, u32[]{:S(2)}) copy-start(bf16[8,256,768]{2,1,0:T(8,128)(2,1)} %copy-done.25) | copy-start | bytes 9437188
  254.6 10.5 %collective-permute-start.14 = (bf16[2,2,256,768]{3,2,1,0:T(8,128)(2,1)S(1)}, bf16[2,2,256,768]{3,2,1,0:T(8,128)(2,1)S(1)}, u32[]{:S(2)}, u32[]{:S(2)}) collective-permute-start(bf16[2,2,256,768]{3,2,1,0:T(8,128)(2,1)S(1)} %maximum_select_fusion.9), channel_id=1, source_target_pairs={{0,1},{1,0},{2,3},{3,2},{4,5},{5,4},{6,7},{7,6},{8,9},{9,8},{10,11... | collective-permute-start | bytes 4718600 | tf_op jit(solution)/shard_map/ppermute | solution.py:39
  266.3 8.1 %copy-start.9 = (bf16[2,2,2,256,768]{4,3,2,1,0:T(8,128)(2,1)}, bf16[2,2,2,256,768]{4,3,2,1,0:T(8,128)(2,1)S(1)}, u32[]{:S(2)}) copy-start(bf16[2,2,2,256,768]{4,3,2,1,0:T(8,128)(2,1)S(1)} %copy.102) | copy-start | bytes 9437188
  288.8 169.7 %collective-permute-start.17 = (bf16[2,2,256,768]{3,2,1,0:T(8,128)(2,1)}, bf16[2,2,256,768]{3,2,1,0:T(8,128)(2,1)}, u32[]{:S(2)}, u32[]{:S(2)}) collective-permute-start(bf16[2,2,256,768]{3,2,1,0:T(8,128)(2,1)} %fusion.40), channel_id=1, source_target_pairs={{0,1},{1,0},{2,3},{3,2},{4,5},{5,4},{6,7},{7,6},{8,9},{9,8},{10,11... | collective-permute-start | bytes 4718600 | tf_op jit(solution)/shard_map/ppermute | solution.py:59
  309.3 5.5 %copy-start.14 = (f32[2,2,2,73728]{3,2,1,0:T(2,128)S(1)}, f32[2,2,2,73728]{3,2,1,0:T(2,128)}, u32[]{:S(2)}) copy-start(f32[2,2,2,73728]{3,2,1,0:T(2,128)} %reshape.746) | copy-start | bytes 7077892
  313.1 100.3 %collective-permute-start.19 = (bf16[2,2,73728]{2,1,0:T(2,128)(2,1)S(1)}, bf16[2,2,73728]{2,1,0:T(2,128)(2,1)}, u32[]{:S(2)}, u32[]{:S(2)}) collective-permute-start(bf16[2,2,73728]{2,1,0:T(2,128)(2,1)S(1)} %bitcast.327), channel_id=1, source_target_pairs={{0,4},{4,0},{8,12},{12,8},{16,20},{20,16},{24,28},{28,24},{1,5},{5... | collective-permute-start | bytes 1769480 | tf_op jit(solution)/shard_map/ppermute | solution.py:99
  410.6 25.3 %slice-start.6 = ((s8[6291456]{0:T(1024)(128)(4,1)}), s8[4194304]{0:T(1024)(128)(4,1)S(1)}, s32[]{:S(2)}) async-start(s8[6291456]{0:T(1024)(128)(4,1)} %bitcast.289), calls=%async_computation.7 | async-start | bytes 8388608
  413.4 22.6 %slice-start.7 = ((s8[6291456]{0:T(1024)(128)(4,1)}), s8[2097152]{0:T(1024)(128)(4,1)S(1)}, s32[]{:S(2)}) async-start(s8[6291456]{0:T(1024)(128)(4,1)} %bitcast.289), calls=%async_computation.8 | async-start | bytes 4194304
  417.1 8.6 %collective-permute-start.20 = (bf16[2,73728]{1,0:T(2,128)(2,1)S(1)}, bf16[2,73728]{1,0:T(2,128)(2,1)S(1)}, u32[]{:S(2)}, u32[]{:S(2)}) collective-permute-start(bf16[2,73728]{1,0:T(2,128)(2,1)S(1)} %bitcast.328), channel_id=1, source_target_pairs={{0,8},{4,12},{8,0},{12,4},{16,24},{20,28},{24,16},{28,20},{1,9},{5... | collective-permute-start | bytes 884744 | tf_op jit(solution)/shard_map/ppermute | solution.py:99
  417.1 41.3 %slice-start.8 = ((s8[6291456]{0:T(1024)(128)(4,1)}), s8[4194304]{0:T(1024)(128)(4,1)S(1)}, s32[]{:S(2)}) async-start(s8[6291456]{0:T(1024)(128)(4,1)} %bitcast.293), calls=%async_computation.9 | async-start | bytes 8388608
  427.1 8.7 %collective-permute-start.21 = (bf16[73728]{0:T(1024)(128)(2,1)S(1)}, bf16[73728]{0:T(1024)(128)(2,1)S(1)}, u32[]{:S(2)}, u32[]{:S(2)}) collective-permute-start(bf16[73728]{0:T(1024)(128)(2,1)S(1)} %convert_reduce_fusion.1), channel_id=1, source_target_pairs={{0,16},{4,20},{8,24},{12,28},{16,0},{20,4},{24,8},{28,12},{1,17},{... | collective-permute-start | bytes 442376 | tf_op jit(solution)/shard_map/ppermute | solution.py:99
  435.8 8.5 %collective-permute-start.22 = (bf16[73728]{0:T(1024)(128)(2,1)S(1)}, bf16[73728]{0:T(1024)(128)(2,1)S(1)}, u32[]{:S(2)}, u32[]{:S(2)}) collective-permute-start(bf16[73728]{0:T(1024)(128)(2,1)S(1)} %add_convert_fusion.2), channel_id=1, source_target_pairs={{0,16},{4,20},{8,24},{12,28},{16,0},{20,4},{24,8},{28,12},{1,17},{... | collective-permute-start | bytes 442376 | tf_op jit(solution)/shard_map/ppermute | solution.py:105
  435.9 22.5 %slice-start.9 = ((s8[6291456]{0:T(1024)(128)(4,1)}), s8[2097152]{0:T(1024)(128)(4,1)S(1)}, s32[]{:S(2)}) async-start(s8[6291456]{0:T(1024)(128)(4,1)} %bitcast.293), calls=%async_computation.10 | async-start | bytes 4194304
  436.1 26.7 %collective-permute-start.15 = (bf16[2,2,256,768]{3,2,1,0:T(8,128)(2,1)S(1)}, bf16[2,2,256,768]{3,2,1,0:T(8,128)(2,1)S(1)}, u32[]{:S(2)}, u32[]{:S(2)}) collective-permute-start(bf16[2,2,256,768]{3,2,1,0:T(8,128)(2,1)S(1)} %fusion.39), channel_id=1, source_target_pairs={{0,1},{1,0},{2,3},{3,2},{4,5},{5,4},{6,7},{7,6},{8,9},{9,8},{10,11... | collective-permute-start | bytes 4718600 | tf_op jit(solution)/shard_map/ppermute | solution.py:59
  445.8 9.0 %collective-permute-start.23 = (bf16[2,73728]{1,0:T(2,128)(2,1)S(1)}, bf16[2,73728]{1,0:T(2,128)(2,1)S(1)}, u32[]{:S(2)}, u32[]{:S(2)}) collective-permute-start(bf16[2,73728]{1,0:T(2,128)(2,1)S(1)} %broadcast_select_fusion.3), channel_id=1, source_target_pairs={{0,8},{4,12},{8,0},{12,4},{16,24},{20,28},{24,16},{28,20},{1,9},{5... | collective-permute-start | bytes 884744 | tf_op jit(solution)/shard_map/ppermute | solution.py:105
  455.7 14.6 %collective-permute-start.24 = (bf16[2,2,73728]{2,0,1:T(2,128)(2,1)S(1)}, bf16[2,2,73728]{2,0,1:T(2,128)(2,1)S(1)}, u32[]{:S(2)}, u32[]{:S(2)}) collective-permute-start(bf16[2,2,73728]{2,0,1:T(2,128)(2,1)S(1)} %broadcast_select_fusion.1), channel_id=1, source_target_pairs={{0,4},{4,0},{8,12},{12,8},{16,20},{20,16},{24,28},{28,24},{1,5},{5... | collective-permute-start | bytes 1769480 | tf_op jit(solution)/shard_map/ppermute | solution.py:105
  461.4 20.7 %collective-permute-start.18 = (bf16[2,256,768]{2,1,0:T(8,128)(2,1)}, bf16[2,256,768]{2,1,0:T(8,128)(2,1)}, u32[]{:S(2)}, u32[]{:S(2)}) collective-permute-start(bf16[2,256,768]{2,1,0:T(8,128)(2,1)} %fusion.87), channel_id=1, source_target_pairs={{0,2},{1,3},{2,0},{3,1},{4,6},{5,7},{6,4},{7,5},{8,10},{9,11},{10,... | collective-permute-start | bytes 2359304 | tf_op jit(solution)/shard_map/ppermute | solution.py:63
  463.2 10.1 %copy-start.11 = (f32[2,2,256,768]{3,2,1,0:T(8,128)}, f32[2,2,256,768]{3,2,1,0:T(8,128)S(1)}, u32[]{:S(2)}) copy-start(f32[2,2,256,768]{3,2,1,0:T(8,128)S(1)} %bitcast_add_fusion.1) | copy-start | bytes 9437188
  464.2 45.6 %collective-permute-start.16 = (bf16[2,256,768]{2,1,0:T(8,128)(2,1)}, bf16[2,256,768]{2,1,0:T(8,128)(2,1)}, u32[]{:S(2)}, u32[]{:S(2)}) collective-permute-start(bf16[2,256,768]{2,1,0:T(8,128)(2,1)} %fusion.86), channel_id=1, source_target_pairs={{0,2},{1,3},{2,0},{3,1},{4,6},{5,7},{6,4},{7,5},{8,10},{9,11},{10,... | collective-permute-start | bytes 2359304 | tf_op jit(solution)/shard_map/ppermute | solution.py:63
  473.3 8.8 %copy-start.3 = (bf16[2,256,768]{2,1,0:T(8,128)(2,1)S(1)}, bf16[2,256,768]{2,1,0:T(8,128)(2,1)}, u32[]{:S(2)}) copy-start(bf16[2,256,768]{2,1,0:T(8,128)(2,1)} %param.13) | copy-start | bytes 2359300
  473.3 8.8 %copy-start.39 = (f32[768]{0:T(1024)S(1)}, f32[768]{0:T(1024)}, u32[]{:S(2)}) copy-start(f32[768]{0:T(1024)} %param.22) | copy-start | bytes 9220
  473.3 8.8 %copy-start.41 = (f32[2,256]{1,0:T(2,128)S(1)}, f32[2,256]{1,0:T(2,128)}, u32[]{:S(2)}) copy-start(f32[2,256]{1,0:T(2,128)} %copy-done.40) | copy-start | bytes 6148
  486.4 6.0 %collective-permute-start.25 = (f32[4,768]{1,0:T(4,128)S(1)}, f32[4,768]{1,0:T(4,128)S(1)}, u32[]{:S(2)}, u32[]{:S(2)}) collective-permute-start(f32[4,768]{1,0:T(4,128)S(1)} %pad_maximum_fusion.4), channel_id=1, source_target_pairs={{0,1},{1,0},{2,3},{3,2},{4,5},{5,4},{6,7},{7,6},{8,9},{9,8},{10,11... | collective-permute-start | bytes 36872 | tf_op jit(solution)/shard_map/ppermute | solution.py:77
  492.3 7.6 %collective-permute-start.26 = (f32[4,768]{1,0:T(4,128)S(1)}, f32[4,768]{1,0:T(4,128)S(1)}, u32[]{:S(2)}, u32[]{:S(2)}) collective-permute-start(f32[4,768]{1,0:T(4,128)S(1)} %fusion.99), channel_id=1, source_target_pairs={{0,2},{1,3},{2,0},{3,1},{4,6},{5,7},{6,4},{7,5},{8,10},{9,11},{10,... | collective-permute-start | bytes 36872 | tf_op jit(solution)/shard_map/ppermute | solution.py:77
  499.9 3.8 collective-permute-start.27
  503.7 6.1 %copy-start.12 = (f32[2,2,256,768]{3,2,1,0:T(8,128)S(1)}, f32[2,2,256,768]{3,2,1,0:T(8,128)}, u32[]{:S(2)}) copy-start(f32[2,2,256,768]{3,2,1,0:T(8,128)} %copy-done.11) | copy-start | bytes 9437188
  503.7 3.9 collective-permute-start.28
  507.6 4.7 collective-permute-start.29
  (36 other events, 102.1 us)
Sparse Core Ops, SparseCore 0:
  235.6 170.5 all-reduce.2

commit v4 on v3

--- a/solution.py
+++ b/solution.py
@@ -181,9 +181,20 @@
     )
     head_mix = head_mix.reshape(group_rows, slots, heads_local * HD).astype(jnp.bfloat16)
     picked = head_mix
-    attn_local = scatter_rows_mp(
-        jnp.einsum("rsk,kd->rsd", picked, out_weight, preferred_element_type=jnp.float32)
-    )
+    attn_partial = jnp.einsum("rsk,kd->rsd", picked, out_weight, preferred_element_type=jnp.float32)
+    count_float = counts.astype(jnp.float32)
+    loss_weight = jnp.sum(count_float) / (experts * count_float)
+    local_hot = lax.dynamic_slice_in_dim(expert_hot, first_row, local_rows, 0)
+    row_weight = jnp.sum(jnp.where(local_hot, loss_weight[None, :], 0.0), axis=1)
+    live_local = lax.dynamic_slice_in_dim(live_mask, first_row, local_rows, 0)
+    grad_output = (
+        cotangent.astype(jnp.float32)
+        * live_local[:, :, None].astype(jnp.float32)
+        * row_weight[:, None, None]
+    )
+    grad_ffn_full = gather_rows_mp(grad_output.astype(jnp.bfloat16))
+    grad_ffn_full, attn_partial = lax.optimization_barrier((grad_ffn_full, attn_partial))
+    attn_local = scatter_rows_mp(attn_partial)
     residual = token_float + attn_local
     norm_two = layer_norm(residual, gain_ffn, shift_ffn).astype(jnp.bfloat16)
     norm_two_full = gather_rows_mp(norm_two)
@@ -207,17 +218,6 @@
             preferred_element_type=jnp.float32,
         )
     ffn_partial = total
-    count_float = counts.astype(jnp.float32)
-    loss_weight = jnp.sum(count_float) / (experts * count_float)
-    local_hot = lax.dynamic_slice_in_dim(expert_hot, first_row, local_rows, 0)
-    row_weight = jnp.sum(jnp.where(local_hot, loss_weight[None, :], 0.0), axis=1)
-    live_local = lax.dynamic_slice_in_dim(live_mask, first_row, local_rows, 0)
-    grad_output = (
-        cotangent.astype(jnp.float32)
-        * live_local[:, :, None].astype(jnp.float32)
-        * row_weight[:, None, None]
-    )
-    grad_ffn_full = gather_rows_mp(grad_output.astype(jnp.bfloat16))
     grad_act = jnp.zeros(upward.shape, jnp.float32)
     down_list = []
     for expert in range(experts):
@@ -312,7 +312,10 @@
         ),
         "dp",
     )
-    attn_summed = butterfly_allreduce_low((grad_qkv_weight, grad_out_weight), "dp")
+    attn_grads, ffn_summed = lax.optimization_barrier(
+        ((grad_qkv_weight, grad_out_weight), ffn_summed)
+    )
+    attn_summed = butterfly_allreduce_low(attn_grads, "dp")
     summed = attn_summed + tuple(g.astype(jnp.float32) for g in ffn_summed)
     return (
         output,

time: 524 us -> 561 us (1.071)
  waiting for transfers between devices: 232 us -> 254 us
  other arithmetic: 101 us -> 111 us
    psum x1, waiting for transfers between devices: 89.3 us -> 109 us  [per_device(): ffn_summed = lax.psum(ffn_grads, 'dp')]
    select_n x2 -> x3, other arithmetic: 3.53 us -> 14.4 us  [gather_rows_mp(): jnp.where(core == 0, jnp.stack([pair, other_core], axis=1), jnp.stack([ot...]
    ppermute x4, waiting for transfers between devices: 60.6 us -> 54.1 us  [gather_rows_mp(): other_y = lax.ppermute(values, 'mp', xor_pairs(4, 2))]
    unnamed x141 -> x119, local copies, waits for them, and re-layouts: 22 us -> 15.9 us
  transfers between devices with their start and end apart: 31 -> 31, of which waited for: 20 -> 21; matrix products, arithmetic and copies ran while one was open for 24% -> 26% of each run, Pallas kernels for 0% -> 0%
where the time goes in v4:
time: 561 us; the launch traced here: 552 us
  waiting for transfers between devices  254 us (45%)
  other arithmetic  111 us (20%)
  matrix products  81.7 us (15%)
  local copies, waits for them, and re-layouts  58.3 us (10%)
  starting transfers between devices  30.5 us (5%)
  between operations  15.7 us (3%)
    psum x1, waiting for transfers between devices, per_device(): ffn_summed = lax.psum(ffn_grads, 'dp')  109 us
    ppermute x4, waiting for transfers between devices, gather_rows_mp(): other_y = lax.ppermute(values, 'mp', xor_pairs(4, 2))  54.1 us
    ppermute x4, waiting for transfers between devices, scatter_rows_mp(): got_y = lax.ppermute(send_y.astype(jnp.bfloat16), 'mp', xor_pairs(4, 2))  38.1 us
    ppermute x3, waiting for transfers between devices, butterfly_allreduce_low(): got = lax.ppermute(send.astype(jnp.bfloat16), axis, xor_pairs(size, bit))  20.1 us
    ppermute x3, waiting for transfers between devices, butterfly_allreduce_low(): got = lax.ppermute(held, axis, xor_pairs(size, bit))  18.9 us
    dot_general x2, matrix products, per_device(): jnp.einsum('rsd,fd->rsf', masked_grad, down_weight[expert], preferred_ele...  18 us
    unnamed x119, local copies, waits for them, and re-layouts  15.9 us
    select_n x8, other arithmetic, gather_rows_mp(): jnp.where(chip_y == 0, jnp.stack([values, other_y]), jnp.stack([other_y,...  14.5 us
  transfers between devices with their start and end apart: 31, of which 21 were waited for; matrix products, arithmetic and copies ran while one was open for 26% of the time, Pallas kernels for 0%

profile of v4, /device:TPU:0, one launch (start us, length us, event | category | flops | bytes accessed | tf_op | source)
XLA Modules:
  0.0 551.9 jit_solution(399847293524956022)
XLA Ops:
  10.3 2.4 fusion.47
  12.7 3.0 collective-permute-start.5
  21.1 2.0 collective-permute-done.1
  23.1 2.6 collective-permute-start.2
  28.8 4.7 collective-permute-done.5
  33.5 3.3 maximum_select_fusion.6
  43.3 15.0 %collective-permute-done.3 = bf16[2,256,768]{2,1,0:T(8,128)(2,1)} collective-permute-done((bf16[2,256,768]{2,1,0:T(8,128)(2,1)}, bf16[2,256,768]{2,1,0:T(8,128)(2,1)}, u32[]{:S(2)}, u32[]{:S(2)}) %collective-permute-start.3) | collective-permute-done | bytes 786464 | tf_op jit(solution)/shard_map/ppermute | solution.py:35
  61.7 2.4 maximum_select_fusion.1
  64.4 2.0 convolution_convert_fusion
  72.8 11.1 %maximum_select_fusion = bf16[2,2,2,256,768]{4,3,2,0,1:T(8,128)(2,1)S(1)} fusion(bf16[2,1,2,256,768]{4,3,2,0,1:T(8,128)(2,1)S(1)} %bitcast.314, bf16[2,1,2,256,768]{4,3,2,0,1:T(8,128)(2,1)S(1)} %fusion.55, pred[]{:T(512)S(6)} %eq.90), kind=kLoop, calls=%fused_computation.31 | loop fusion | flops 4718592 | bytes 6291457 | tf_op jit(solution)/shard_map/jit(_where)/select_n | solution.py:40
  86.4 3.2 collective-permute-done.7
  89.6 2.7 bitcast_add_fusion.3
  95.8 18.2 %collective-permute-done.8 = bf16[2,256,768]{2,1,0:T(8,128)(2,1)} collective-permute-done((bf16[2,256,768]{2,1,0:T(8,128)(2,1)S(1)}, bf16[2,256,768]{2,1,0:T(8,128)(2,1)}, u32[]{:S(2)}, u32[]{:S(2)}) %collective-permute-start.8) | collective-permute-done | bytes 786464 | tf_op jit(solution)/shard_map/ppermute | solution.py:63
  114.0 2.0 fusion.119
  118.8 16.9 %collective-permute-done.9 = bf16[2,256,768]{2,1,0:T(8,128)(2,1)S(1)} collective-permute-done((bf16[2,256,768]{2,1,0:T(8,128)(2,1)S(1)}, bf16[2,256,768]{2,1,0:T(8,128)(2,1)S(1)}, u32[]{:S(2)}, u32[]{:S(2)}) %collective-permute-start.9) | collective-permute-done | bytes 786464 | tf_op jit(solution)/shard_map/ppermute | solution.py:35
  137.3 7.5 %fusion.22 = f32[8,256,768]{2,1,0:T(8,128)} fusion(bf16[8,256,768]{2,1,0:T(8,128)(2,1)} %bitcast.295, bf16[8]{0:T(256)(128)(2,1)S(1)} %get-tuple-element.86, bf16[2,768,768]{2,1,0:T(8,128)(2,1)} %param.21), kind=kOutput, calls=%fused_computation.57 | convolution fusion | flops 2417491968 | bytes 10616848 | tf_op jit(solution)/shard_map/rsd,fd->rsf/dot_general | solution.py:225
  146.2 2.7 broadcast_multiply_fusion
  151.3 2.7 fusion.89
  154.0 4.5 fusion.69
  158.5 14.4 %multiply_convert_fusion.1 = (bf16[8,256,768]{2,1,0:T(8,128)(2,1)S(1)}, f32[8,256,768]{2,1,0:T(8,128)S(1)}) fusion(f32[8,256,768]{2,1,0:T(8,128)S(1)} %get-tuple-element.93, u8[256,768]{1,0:T(8,128)(4,1)S(1)} %get-tuple-element.56, u8[256,768]{1,0:T(8,128)(4,1)S(1)} %get-tuple-element.55), kind=kLoop, calls=%fused_computation.11 | loop fusion | flops 110100480 | bytes 16121856 | tf_op jit(solution)/shard_map/convert_element_type | solution.py:209
  172.9 2.8 fusion.76
  175.8 3.8 fusion.73
  179.6 3.3 bitcast_multiply_fusion.1
  182.8 10.5 %add_convert_fusion = bf16[8,256,768]{2,1,0:T(8,128)(2,1)} fusion(f32[8,256,768]{2,1,0:T(8,128)S(1)} %get-tuple-element.76, f32[8,256,768]{2,1,0:T(8,128)} %fusion.22, f32[8,256,768]{2,1,0:T(8,128)S(1)} %get-tuple-element.93, bf16[8,256,768]{2,1,0:T(8,128)(2,1)} %bitcast.296, bf16[8]{0:T(256)(128)(2,1)S(1)} %get-tuple-element.85, ...), kind=kOutput, calls=%fused_computation.10 | convolution fusion | flops 2441084928 | bytes 26345488 | tf_op jit(solution)/shard_map/rsd,fd->rsf/dot_general | solution.py:225
  193.4 5.8 %fusion.79 = bf16[1,768,768]{2,1,0:T(8,128)(2,1)S(1)} fusion(bf16[8,256,768]{2,1,0:T(8,128)(2,1)} %get-tuple-element.83, bf16[8,256,768]{2,1,0:T(8,128)(2,1)} %add_convert_fusion), kind=kOutput, calls=%fused_computation.145 | convolution fusion | flops 2416508928 | bytes 7471104 | tf_op jit(solution)/shard_map/rsd,rsf->df/dot_general | solution.py:236
  199.3 2.8 fusion.80
  202.1 2.4 pad_maximum_fusion
  204.5 5.1 fusion.11
  209.6 2.7 fusion.35
  213.1 3.0 collective-permute-done.11
  218.4 18.1 %collective-permute-done.12 = bf16[2,256,768]{2,1,0:T(8,128)(2,1)S(1)} collective-permute-done((bf16[2,256,768]{2,1,0:T(8,128)(2,1)S(1)}, bf16[2,256,768]{2,1,0:T(8,128)(2,1)S(1)}, u32[]{:S(2)}, u32[]{:S(2)}) %collective-permute-start.12) | collective-permute-done | bytes 786464 | tf_op jit(solution)/shard_map/ppermute | solution.py:63
  241.4 17.5 %collective-permute-done.13 = bf16[2,256,768]{2,1,0:T(8,128)(2,1)} collective-permute-done((bf16[2,256,768]{2,1,0:T(8,128)(2,1)}, bf16[2,256,768]{2,1,0:T(8,128)(2,1)}, u32[]{:S(2)}, u32[]{:S(2)}) %collective-permute-start.13) | collective-permute-done | bytes 786464 | tf_op jit(solution)/shard_map/ppermute | solution.py:35
  258.9 2.3 maximum_select_fusion.9
  261.3 4.1 fusion.15
  265.4 4.7 fusion.32
  270.1 2.3 fusion.56
  276.0 5.3 multiply_reduce_fusion
  281.2 4.5 multiply_convert_fusion
  287.6 2.2 multiply_bitcast_fusion
  291.5 2.7 fusion.121
  299.3 3.3 convolution_bitcast_fusion
  302.6 108.8 %all-reduce.3.cloned.1.call-done = (bf16[2,768,768]{2,1,0:T(8,128)(2,1)}, bf16[2,768,768]{2,1,0:T(8,128)(2,1)}) async-done(((bf16[2,768,768]{2,1,0:T(8,128)(2,1)}, bf16[2,768,768]{2,1,0:T(8,128)(2,1)}), (bf16[2,768,768]{2,1,0:T(8,128)(2,1)}, bf16[2,768,768]{2,1,0:T(8,128)(2,1)})) %all-reduce.3.cloned.1.call-update) | async-done | bytes 4718608 | tf_op jit(solution)/shard_map/psum | solution.py:246
  411.4 4.2 copy.114
  415.6 4.7 reshape.696
  422.1 3.2 pad_maximum_fusion.2
  425.4 4.7 reshape.698
  430.1 2.9 dynamic-slice_convert_fusion.5
  436.7 2.5 convert_element_type.253
  439.2 2.8 convert_element_type.254
  442.0 6.9 %collective-permute-done.19 = bf16[2,2,73728]{2,1,0:T(2,128)(2,1)S(1)} collective-permute-done((bf16[2,2,73728]{2,1,0:T(2,128)(2,1)S(1)}, bf16[2,2,73728]{2,1,0:T(2,128)(2,1)S(1)}, u32[]{:S(2)}, u32[]{:S(2)}) %collective-permute-start.19) | collective-permute-done | bytes 589856 | tf_op jit(solution)/shard_map/ppermute | solution.py:99
  451.7 7.1 %collective-permute-done.20 = bf16[2,73728]{1,0:T(2,128)(2,1)S(1)} collective-permute-done((bf16[2,73728]{1,0:T(2,128)(2,1)S(1)}, bf16[2,73728]{1,0:T(2,128)(2,1)S(1)}, u32[]{:S(2)}, u32[]{:S(2)}) %collective-permute-start.20) | collective-permute-done | bytes 294944 | tf_op jit(solution)/shard_map/ppermute | solution.py:99
  461.9 6.1 %collective-permute-done.21 = bf16[73728]{0:T(1024)(128)(2,1)S(1)} collective-permute-done((bf16[73728]{0:T(1024)(128)(2,1)S(1)}, bf16[73728]{0:T(1024)(128)(2,1)S(1)}, u32[]{:S(2)}, u32[]{:S(2)}) %collective-permute-start.21) | collective-permute-done | bytes 147488 | tf_op jit(solution)/shard_map/ppermute | solution.py:99
  468.7 7.7 %collective-permute-done.22 = bf16[73728]{0:T(1024)(128)(2,1)S(1)} collective-permute-done((bf16[73728]{0:T(1024)(128)(2,1)S(1)}, bf16[73728]{0:T(1024)(128)(2,1)S(1)}, u32[]{:S(2)}, u32[]{:S(2)}) %collective-permute-start.22) | collective-permute-done | bytes 147488 | tf_op jit(solution)/shard_map/ppermute | solution.py:105
  481.0 5.9 %collective-permute-done.23 = bf16[2,73728]{1,0:T(2,128)(2,1)S(1)} collective-permute-done((bf16[2,73728]{1,0:T(2,128)(2,1)S(1)}, bf16[2,73728]{1,0:T(2,128)(2,1)S(1)}, u32[]{:S(2)}, u32[]{:S(2)}) %collective-permute-start.23) | collective-permute-done | bytes 294944 | tf_op jit(solution)/shard_map/ppermute | solution.py:105
  496.9 5.3 collective-permute-done.24
  505.2 2.2 copy.118
  507.4 4.6 select_n.356
  513.9 2.1 fusion.50
  518.3 2.1 slice_convert_fusion
  520.3 3.7 select_n.357
  527.4 4.2 copy.120
  532.3 3.1 collective-permute-done.27
  535.8 3.6 add_add_fusion.2
  540.8 2.4 fusion.58
  (273 shorter events, 103.0 us)
Async XLA Ops:
  7.2 57.2 %copy-start = (bf16[768,3,192]{0,2,1:T(8,128)(2,1)S(1)}, bf16[768,3,192]{0,2,1:T(8,128)(2,1)}, u32[]{:S(2)}) copy-start(bf16[768,3,192]{0,2,1:T(8,128)(2,1)} %param.18) | copy-start | bytes 2654212
  7.2 10.3 %copy-start.2 = (bf16[2,256,768]{2,1,0:T(8,128)(2,1)S(1)}, bf16[2,256,768]{2,1,0:T(8,128)(2,1)}, u32[]{:S(2)}) copy-start(bf16[2,256,768]{2,1,0:T(8,128)(2,1)} %param.13) | copy-start | bytes 2359300
  7.2 10.2 %copy-start.32 = (f32[768]{0:T(1024)S(1)}, f32[768]{0:T(1024)}, u32[]{:S(2)}) copy-start(f32[768]{0:T(1024)} %param.22) | copy-start | bytes 9220
  7.2 10.2 %copy-start.40 = (f32[768]{0:T(1024)S(1)}, f32[768]{0:T(1024)}, u32[]{:S(2)}) copy-start(f32[768]{0:T(1024)} %param.23) | copy-start | bytes 9220
  7.2 8.4 %copy-start.39 = (s32[8,256]{1,0:T(8,128)S(1)}, s32[8,256]{1,0:T(8,128)}, u32[]{:S(2)}) copy-start(s32[8,256]{1,0:T(8,128)} %param.16) | copy-start | bytes 24580
  7.2 8.5 %copy-start.49 = (s32[8]{0:T(128)S(1)}, s32[8]{0:T(128)}, u32[]{:S(2)}) copy-start(s32[8]{0:T(128)} %param.17) | copy-start | bytes 100
  7.2 404.1 %all-reduce.3.cloned.1.call-start = ((), (), s32[]{:S(2)}) async-start(), calls=%async_computation | async-start | bytes 9437184 | tf_op jit(solution)/shard_map/psum | solution.py:246
  8.7 10.4 %copy-start.34 = (f32[2,256]{1,0:T(2,128)}, f32[2,256]{1,0:T(2,128)S(1)}, u32[]{:S(2)}) copy-start(f32[2,256]{1,0:T(2,128)S(1)} %broadcast_multiply_fusion.3) | copy-start | bytes 6148
  10.2 8.5 %copy-start.43 = (f32[2,256]{1,0:T(2,128)}, f32[2,256]{1,0:T(2,128)S(1)}, u32[]{:S(2)}) copy-start(f32[2,256]{1,0:T(2,128)S(1)} %fusion.49) | copy-start | bytes 6148
  10.3 8.9 %copy-start.37 = (f32[2,256]{1,0:T(2,128)}, f32[2,256]{1,0:T(2,128)S(1)}, u32[]{:S(2)}) copy-start(f32[2,256]{1,0:T(2,128)S(1)} %fusion.111) | copy-start | bytes 6148
  12.7 20.8 %collective-permute-start.5 = (bf16[2,256,768]{2,1,0:T(8,128)(2,1)}, bf16[2,256,768]{2,1,0:T(8,128)(2,1)}, u32[]{:S(2)}, u32[]{:S(2)}) collective-permute-start(bf16[2,256,768]{2,1,0:T(8,128)(2,1)} %fusion.47), channel_id=1, source_target_pairs={{0,2},{1,3},{2,0},{3,1},{4,6},{5,7},{6,4},{7,5},{8,10},{9,11},{10,... | collective-permute-start | bytes 2359304 | tf_op jit(solution)/shard_map/ppermute | solution.py:35
  15.9 3.6 collective-permute-start
  18.8 18.2 %copy-start.3 = (bf16[2,256,768]{2,1,0:T(8,128)(2,1)S(1)}, bf16[2,256,768]{2,1,0:T(8,128)(2,1)}, u32[]{:S(2)}) copy-start(bf16[2,256,768]{2,1,0:T(8,128)(2,1)} %param.14) | copy-start | bytes 2359300
  19.5 3.6 collective-permute-start.1
  23.1 4.5 collective-permute-start.2
  28.2 8.7 %copy-start.45 = (s32[2]{0:T(128)}, s32[2]{0:T(128)S(1)}, u32[]{:S(2)}) copy-start(s32[2]{0:T(128)S(1)} %get-tuple-element.82) | copy-start | bytes 28
  33.5 6.3 %copy-start.42 = (s32[8,256]{1,0:T(8,128)S(1)}, s32[8,256]{1,0:T(8,128)}, u32[]{:S(2)}) copy-start(s32[8,256]{1,0:T(8,128)} %param.15) | copy-start | bytes 24580
  36.8 24.9 %collective-permute-start.6 = (bf16[2,2,256,768]{3,2,1,0:T(8,128)(2,1)}, bf16[2,2,256,768]{3,2,1,0:T(8,128)(2,1)}, u32[]{:S(2)}, u32[]{:S(2)}) collective-permute-start(bf16[2,2,256,768]{3,2,1,0:T(8,128)(2,1)} %maximum_select_fusion.6), channel_id=1, source_target_pairs={{0,1},{1,0},{2,3},{3,2},{4,5},{5,4},{6,7},{7,6},{8,9},{9,8},{10,11... | collective-permute-start | bytes 4718600 | tf_op jit(solution)/shard_map/ppermute | solution.py:39
  38.1 20.3 %collective-permute-start.3 = (bf16[2,256,768]{2,1,0:T(8,128)(2,1)}, bf16[2,256,768]{2,1,0:T(8,128)(2,1)}, u32[]{:S(2)}, u32[]{:S(2)}) collective-permute-start(bf16[2,256,768]{2,1,0:T(8,128)(2,1)} %fusion.67), channel_id=1, source_target_pairs={{0,2},{1,3},{2,0},{3,1},{4,6},{5,7},{6,4},{7,5},{8,10},{9,11},{10,... | collective-permute-start | bytes 2359304 | tf_op jit(solution)/shard_map/ppermute | solution.py:35
  60.0 12.8 %collective-permute-start.4 = (bf16[2,2,256,768]{3,2,1,0:T(8,128)(2,1)S(1)}, bf16[2,2,256,768]{3,2,1,0:T(8,128)(2,1)S(1)}, u32[]{:S(2)}, u32[]{:S(2)}) collective-permute-start(bf16[2,2,256,768]{3,2,1,0:T(8,128)(2,1)S(1)} %maximum_select_fusion.4), channel_id=1, source_target_pairs={{0,1},{1,0},{2,3},{3,2},{4,5},{5,4},{6,7},{7,6},{8,9},{9,8},{10,11... | collective-permute-start | bytes 4718600 | tf_op jit(solution)/shard_map/ppermute | solution.py:39
  72.7 13.0 %copy-start.5 = (f32[8,256,768]{2,1,0:T(8,128)}, f32[8,256,768]{2,1,0:T(8,128)S(1)}, u32[]{:S(2)}) copy-start(f32[8,256,768]{2,1,0:T(8,128)S(1)} %fusion.107) | copy-start | bytes 18874372
  85.9 3.7 collective-permute-start.7
  94.0 20.0 %collective-permute-start.8 = (bf16[2,256,768]{2,1,0:T(8,128)(2,1)S(1)}, bf16[2,256,768]{2,1,0:T(8,128)(2,1)}, u32[]{:S(2)}, u32[]{:S(2)}) collective-permute-start(bf16[2,256,768]{2,1,0:T(8,128)(2,1)S(1)} %fusion.100), channel_id=1, source_target_pairs={{0,2},{1,3},{2,0},{3,1},{4,6},{5,7},{6,4},{7,5},{8,10},{9,11},{10,... | collective-permute-start | bytes 2359304 | tf_op jit(solution)/shard_map/ppermute | solution.py:63
  95.8 20.5 %copy-start.36 = (f32[768]{0:T(1024)S(1)}, f32[768]{0:T(1024)}, u32[]{:S(2)}) copy-start(f32[768]{0:T(1024)} %param.24) | copy-start | bytes 9220
  95.8 20.5 %copy-start.41 = (f32[768]{0:T(1024)S(1)}, f32[768]{0:T(1024)}, u32[]{:S(2)}) copy-start(f32[768]{0:T(1024)} %param.25) | copy-start | bytes 9220
  116.7 19.0 %collective-permute-start.9 = (bf16[2,256,768]{2,1,0:T(8,128)(2,1)S(1)}, bf16[2,256,768]{2,1,0:T(8,128)(2,1)S(1)}, u32[]{:S(2)}, u32[]{:S(2)}) collective-permute-start(bf16[2,256,768]{2,1,0:T(8,128)(2,1)S(1)} %add_convert_fusion.1), channel_id=1, source_target_pairs={{0,2},{1,3},{2,0},{3,1},{4,6},{5,7},{6,4},{7,5},{8,10},{9,11},{10,... | collective-permute-start | bytes 2359304 | tf_op jit(solution)/shard_map/ppermute | solution.py:35
  137.1 9.1 %collective-permute-start.10 = (bf16[2,2,256,768]{3,2,1,0:T(8,128)(2,1)}, bf16[2,2,256,768]{3,2,1,0:T(8,128)(2,1)}, u32[]{:S(2)}, u32[]{:S(2)}) collective-permute-start(bf16[2,2,256,768]{3,2,1,0:T(8,128)(2,1)} %maximum_select_fusion.8), channel_id=1, source_target_pairs={{0,1},{1,0},{2,3},{3,2},{4,5},{5,4},{6,7},{7,6},{8,9},{9,8},{10,11... | collective-permute-start | bytes 4718600 | tf_op jit(solution)/shard_map/ppermute | solution.py:39
  158.5 14.5 %copy-start.18 = (bf16[2,2,2,256,768]{4,3,2,1,0:T(8,128)(2,1)S(1)}, bf16[2,2,2,256,768]{4,3,2,1,0:T(8,128)(2,1)}, u32[]{:S(2)}) copy-start(bf16[2,2,2,256,768]{4,3,2,1,0:T(8,128)(2,1)} %copy.86) | copy-start | bytes 9437188
  193.4 5.9 %copy-start.15 = (bf16[8,256,768]{2,1,0:T(8,128)(2,1)S(1)}, bf16[8,256,768]{2,1,0:T(8,128)(2,1)}, u32[]{:S(2)}) copy-start(bf16[8,256,768]{2,1,0:T(8,128)(2,1)} %get-tuple-element.84) | copy-start | bytes 9437188
  193.4 5.9 %copy-start.50 = (bf16[8,256,768]{2,1,0:T(8,128)(2,1)S(1)}, bf16[8,256,768]{2,1,0:T(8,128)(2,1)}, u32[]{:S(2)}) copy-start(bf16[8,256,768]{2,1,0:T(8,128)(2,1)} %add_convert_fusion) | copy-start | bytes 9437188
  204.5 5.1 copy-start.47
  204.5 5.1 copy-start.51
  212.5 3.6 collective-permute-start.11
  216.6 19.9 %collective-permute-start.12 = (bf16[2,256,768]{2,1,0:T(8,128)(2,1)S(1)}, bf16[2,256,768]{2,1,0:T(8,128)(2,1)S(1)}, u32[]{:S(2)}, u32[]{:S(2)}) collective-permute-start(bf16[2,256,768]{2,1,0:T(8,128)(2,1)S(1)} %fusion.101), channel_id=1, source_target_pairs={{0,2},{1,3},{2,0},{3,1},{4,6},{5,7},{6,4},{7,5},{8,10},{9,11},{10,... | collective-permute-start | bytes 2359304 | tf_op jit(solution)/shard_map/ppermute | solution.py:63
  239.6 19.3 %collective-permute-start.13 = (bf16[2,256,768]{2,1,0:T(8,128)(2,1)}, bf16[2,256,768]{2,1,0:T(8,128)(2,1)}, u32[]{:S(2)}, u32[]{:S(2)}) collective-permute-start(bf16[2,256,768]{2,1,0:T(8,128)(2,1)} %fusion.99), channel_id=1, source_target_pairs={{0,2},{1,3},{2,0},{3,1},{4,6},{5,7},{6,4},{7,5},{8,10},{9,11},{10,... | collective-permute-start | bytes 2359304 | tf_op jit(solution)/shard_map/ppermute | solution.py:35
  241.4 19.9 %copy-start.22 = (bf16[8,256,768]{2,1,0:T(8,128)(2,1)S(1)}, bf16[8,256,768]{2,1,0:T(8,128)(2,1)}, u32[]{:S(2)}) copy-start(bf16[8,256,768]{2,1,0:T(8,128)(2,1)} %copy-done.21) | copy-start | bytes 9437188
  261.2 4.2 copy-start.48
  261.2 11.2 %collective-permute-start.14 = (bf16[2,2,256,768]{3,2,1,0:T(8,128)(2,1)S(1)}, bf16[2,2,256,768]{3,2,1,0:T(8,128)(2,1)S(1)}, u32[]{:S(2)}, u32[]{:S(2)}) collective-permute-start(bf16[2,2,256,768]{3,2,1,0:T(8,128)(2,1)S(1)} %maximum_select_fusion.9), channel_id=1, source_target_pairs={{0,1},{1,0},{2,3},{3,2},{4,5},{5,4},{6,7},{7,6},{8,9},{9,8},{10,11... | collective-permute-start | bytes 4718600 | tf_op jit(solution)/shard_map/ppermute | solution.py:39
  295.5 194.8 %collective-permute-start.17 = (bf16[2,2,256,768]{3,2,1,0:T(8,128)(2,1)}, bf16[2,2,256,768]{3,2,1,0:T(8,128)(2,1)}, u32[]{:S(2)}, u32[]{:S(2)}) collective-permute-start(bf16[2,2,256,768]{3,2,1,0:T(8,128)(2,1)} %fusion.51), channel_id=1, source_target_pairs={{0,1},{1,0},{2,3},{3,2},{4,5},{5,4},{6,7},{7,6},{8,9},{9,8},{10,11... | collective-permute-start | bytes 4718600 | tf_op jit(solution)/shard_map/ppermute | solution.py:59
  430.1 5.4 copy-start.12
  433.9 15.0 %collective-permute-start.19 = (bf16[2,2,73728]{2,1,0:T(2,128)(2,1)S(1)}, bf16[2,2,73728]{2,1,0:T(2,128)(2,1)S(1)}, u32[]{:S(2)}, u32[]{:S(2)}) collective-permute-start(bf16[2,2,73728]{2,1,0:T(2,128)(2,1)S(1)} %bitcast.319), channel_id=1, source_target_pairs={{0,4},{4,0},{8,12},{12,8},{16,20},{20,16},{24,28},{28,24},{1,5},{5... | collective-permute-start | bytes 1769480 | tf_op jit(solution)/shard_map/ppermute | solution.py:99
  439.2 28.9 %slice-start.2 = ((s8[6291456]{0:T(1024)(128)(4,1)}), s8[4194304]{0:T(1024)(128)(4,1)S(1)}, s32[]{:S(2)}) async-start(s8[6291456]{0:T(1024)(128)(4,1)} %bitcast.285), calls=%async_computation.3 | async-start | bytes 8388608
  442.0 26.1 %slice-start.3 = ((s8[6291456]{0:T(1024)(128)(4,1)}), s8[2097152]{0:T(1024)(128)(4,1)S(1)}, s32[]{:S(2)}) async-start(s8[6291456]{0:T(1024)(128)(4,1)} %bitcast.285), calls=%async_computation.4 | async-start | bytes 4194304
  450.9 7.8 %collective-permute-start.20 = (bf16[2,73728]{1,0:T(2,128)(2,1)S(1)}, bf16[2,73728]{1,0:T(2,128)(2,1)S(1)}, u32[]{:S(2)}, u32[]{:S(2)}) collective-permute-start(bf16[2,73728]{1,0:T(2,128)(2,1)S(1)} %bitcast.320), channel_id=1, source_target_pairs={{0,8},{4,12},{8,0},{12,4},{16,24},{20,28},{24,16},{28,20},{1,9},{5... | collective-permute-start | bytes 884744 | tf_op jit(solution)/shard_map/ppermute | solution.py:99
  451.0 39.3 %slice-start.4 = ((s8[6291456]{0:T(1024)(128)(4,1)}), s8[4194304]{0:T(1024)(128)(4,1)S(1)}, s32[]{:S(2)}) async-start(s8[6291456]{0:T(1024)(128)(4,1)} %bitcast.289), calls=%async_computation.5 | async-start | bytes 8388608
  460.2 7.8 %collective-permute-start.21 = (bf16[73728]{0:T(1024)(128)(2,1)S(1)}, bf16[73728]{0:T(1024)(128)(2,1)S(1)}, u32[]{:S(2)}, u32[]{:S(2)}) collective-permute-start(bf16[73728]{0:T(1024)(128)(2,1)S(1)} %convert_reduce_fusion.1), channel_id=1, source_target_pairs={{0,16},{4,20},{8,24},{12,28},{16,0},{20,4},{24,8},{28,12},{1,17},{... | collective-permute-start | bytes 442376 | tf_op jit(solution)/shard_map/ppermute | solution.py:99
  468.0 8.4 %collective-permute-start.22 = (bf16[73728]{0:T(1024)(128)(2,1)S(1)}, bf16[73728]{0:T(1024)(128)(2,1)S(1)}, u32[]{:S(2)}, u32[]{:S(2)}) collective-permute-start(bf16[73728]{0:T(1024)(128)(2,1)S(1)} %add_convert_fusion.2), channel_id=1, source_target_pairs={{0,16},{4,20},{8,24},{12,28},{16,0},{20,4},{24,8},{28,12},{1,17},{... | collective-permute-start | bytes 442376 | tf_op jit(solution)/shard_map/ppermute | solution.py:105
  468.1 22.2 %slice-start.5 = ((s8[6291456]{0:T(1024)(128)(4,1)}), s8[2097152]{0:T(1024)(128)(4,1)S(1)}, s32[]{:S(2)}) async-start(s8[6291456]{0:T(1024)(128)(4,1)} %bitcast.289), calls=%async_computation.6 | async-start | bytes 4194304
  468.3 26.3 %collective-permute-start.15 = (bf16[2,2,256,768]{3,2,1,0:T(8,128)(2,1)S(1)}, bf16[2,2,256,768]{3,2,1,0:T(8,128)(2,1)S(1)}, u32[]{:S(2)}, u32[]{:S(2)}) collective-permute-start(bf16[2,2,256,768]{3,2,1,0:T(8,128)(2,1)S(1)} %fusion.54), channel_id=1, source_target_pairs={{0,1},{1,0},{2,3},{3,2},{4,5},{5,4},{6,7},{7,6},{8,9},{9,8},{10,11... | collective-permute-start | bytes 4718600 | tf_op jit(solution)/shard_map/ppermute | solution.py:59
  477.9 9.0 %collective-permute-start.23 = (bf16[2,73728]{1,0:T(2,128)(2,1)S(1)}, bf16[2,73728]{1,0:T(2,128)(2,1)S(1)}, u32[]{:S(2)}, u32[]{:S(2)}) collective-permute-start(bf16[2,73728]{1,0:T(2,128)(2,1)S(1)} %broadcast_select_fusion.3), channel_id=1, source_target_pairs={{0,8},{4,12},{8,0},{12,4},{16,24},{20,28},{24,16},{28,20},{1,9},{5... | collective-permute-start | bytes 884744 | tf_op jit(solution)/shard_map/ppermute | solution.py:105
  487.7 14.5 %collective-permute-start.24 = (bf16[2,2,73728]{2,0,1:T(2,128)(2,1)S(1)}, bf16[2,2,73728]{2,0,1:T(2,128)(2,1)S(1)}, u32[]{:S(2)}, u32[]{:S(2)}) collective-permute-start(bf16[2,2,73728]{2,0,1:T(2,128)(2,1)S(1)} %broadcast_select_fusion.1), channel_id=1, source_target_pairs={{0,4},{4,0},{8,12},{12,8},{16,20},{20,16},{24,28},{28,24},{1,5},{5... | collective-permute-start | bytes 1769480 | tf_op jit(solution)/shard_map/ppermute | solution.py:105
  493.1 20.7 %collective-permute-start.18 = (bf16[2,256,768]{2,1,0:T(8,128)(2,1)}, bf16[2,256,768]{2,1,0:T(8,128)(2,1)}, u32[]{:S(2)}, u32[]{:S(2)}) collective-permute-start(bf16[2,256,768]{2,1,0:T(8,128)(2,1)} %fusion.103), channel_id=1, source_target_pairs={{0,2},{1,3},{2,0},{3,1},{4,6},{5,7},{6,4},{7,5},{8,10},{9,11},{10,... | collective-permute-start | bytes 2359304 | tf_op jit(solution)/shard_map/ppermute | solution.py:63
  494.9 10.2 %copy-start.8 = (f32[2,2,256,768]{3,2,1,0:T(8,128)}, f32[2,2,256,768]{3,2,1,0:T(8,128)S(1)}, u32[]{:S(2)}) copy-start(f32[2,2,256,768]{3,2,1,0:T(8,128)S(1)} %bitcast_add_fusion.1) | copy-start | bytes 9437188
  496.0 44.7 %collective-permute-start.16 = (bf16[2,256,768]{2,1,0:T(8,128)(2,1)}, bf16[2,256,768]{2,1,0:T(8,128)(2,1)}, u32[]{:S(2)}, u32[]{:S(2)}) collective-permute-start(bf16[2,256,768]{2,1,0:T(8,128)(2,1)} %fusion.102), channel_id=1, source_target_pairs={{0,2},{1,3},{2,0},{3,1},{4,6},{5,7},{6,4},{7,5},{8,10},{9,11},{10,... | collective-permute-start | bytes 2359304 | tf_op jit(solution)/shard_map/ppermute | solution.py:63
  505.2 8.7 %copy-start.33 = (f32[768]{0:T(1024)S(1)}, f32[768]{0:T(1024)}, u32[]{:S(2)}) copy-start(f32[768]{0:T(1024)} %param.22) | copy-start | bytes 9220
  505.2 8.7 %copy-start.35 = (f32[2,256]{1,0:T(2,128)S(1)}, f32[2,256]{1,0:T(2,128)}, u32[]{:S(2)}) copy-start(f32[2,256]{1,0:T(2,128)} %copy-done.34) | copy-start | bytes 6148
  512.0 4.0 copy-start.44
  512.0 5.2 copy-start.38
  518.2 5.9 %collective-permute-start.25 = (f32[4,768]{1,0:T(4,128)S(1)}, f32[4,768]{1,0:T(4,128)S(1)}, u32[]{:S(2)}, u32[]{:S(2)}) collective-permute-start(f32[4,768]{1,0:T(4,128)S(1)} %pad_maximum_fusion.3), channel_id=1, source_target_pairs={{0,1},{1,0},{2,3},{3,2},{4,5},{5,4},{6,7},{7,6},{8,9},{9,8},{10,11... | collective-permute-start | bytes 36872 | tf_op jit(solution)/shard_map/ppermute | solution.py:77
  524.1 7.6 %collective-permute-start.26 = (f32[4,768]{1,0:T(4,128)S(1)}, f32[4,768]{1,0:T(4,128)S(1)}, u32[]{:S(2)}, u32[]{:S(2)}) collective-permute-start(f32[4,768]{1,0:T(4,128)S(1)} %fusion.115), channel_id=1, source_target_pairs={{0,2},{1,3},{2,0},{3,1},{4,6},{5,7},{6,4},{7,5},{8,10},{9,11},{10,... | collective-permute-start | bytes 36872 | tf_op jit(solution)/shard_map/ppermute | solution.py:77
  531.7 3.8 collective-permute-start.27
  535.5 5.3 copy-start.9
  535.5 3.9 collective-permute-start.28
  539.4 4.7 collective-permute-start.29
  (25 other events, 55.0 us)
Sparse Core Ops, SparseCore 0:
  241.5 169.7 all-reduce.2
